TPU v7x, 256 devices: a whole 4x4x8 slice. The times are simulated.
256 devices in a mesh: expert: 16 (over z, core), fsdp: 16 (over x, y).
Axes of the slice: x: 4, y: 4, z: 8, core: 2. Of those that a mesh axis runs over, the one named last changes fastest.
Arguments:
- tokens: bfloat16 [4096, 6144], P(('expert', 'fsdp')), may hold values from -6 to 6
- expert_ids: int32 [4096, 4], P(('expert', 'fsdp')), may hold values from 0 to 15, all different within a row; in each aligned block of 16 rows (0 to 15, 16 to 31, ...) at most 5 rows name the same one
- router_weight: float32 [4096, 4], P(('expert', 'fsdp')), may hold values from 0.1 to 1
- w_gate: bfloat16 [16, 5376, 6144], P('expert', 'fsdp'), may hold values from -0.078125 to 0.078125
- w_up: bfloat16 [16, 5376, 6144], P('expert', 'fsdp'), may hold values from -0.078125 to 0.078125
Outputs:
- routed: bfloat16 [4096, 4, 5376], P(('expert', 'fsdp'))
Inputs may be any that keep to these rules, and one draw needn't show every extreme that they name: `expert_ids`: each row names 4 different experts; the 16 rows of one device name any one expert at most 5 times, and some device names some expert exactly 5 times.
All inputs are finite; a program needn't handle non-finite values.
Results may differ from a plain program's by a relative error of at most 0.0049.
Values may be sent and summed in bfloat16 or wider, within the bound.
No kernel may reach another device: no remote copies, remote signals or barrier semaphores. Data moves between devices by JAX's collectives and lax.ppermute only.
A program may use at most 128 MiB of HBM per device.

v0:
```python
import jax
import jax.numpy as jnp
from jax import lax
from jax.sharding import PartitionSpec as P


def hidden_block(row_block, gate_rows, up_rows):
    gate_act = lax.dot_general(
        row_block, gate_rows, (((1,), (1,)), ((), ())), preferred_element_type=jnp.float32
    )
    up_act = lax.dot_general(
        row_block, up_rows, (((1,), (1,)), ((), ())), preferred_element_type=jnp.float32
    )
    return (jax.nn.gelu(gate_act, approximate=False) * up_act).astype(jnp.bfloat16)


def local(tokens, expert_ids, router_weight, w_gate, w_up):
    tok_rows, model_width = tokens.shape
    top_count = expert_ids.shape[1]
    experts = lax.axis_size("expert")
    fsdp_size = lax.axis_size("fsdp")
    cap_slots = 5 * tok_rows * top_count // (4 * experts)
    flat_ids = expert_ids.reshape(-1)
    choosing = (flat_ids[:, None] == jnp.arange(experts, dtype=jnp.int32)[None, :]).astype(
        jnp.int32
    )
    slot_rank = jnp.sum((jnp.cumsum(choosing, axis=0) - 1) * choosing, axis=1)
    slot_of = flat_ids * cap_slots + slot_rank
    placing = (
        slot_of[None, :] == jnp.arange(experts * cap_slots, dtype=jnp.int32)[:, None]
    ).astype(jnp.bfloat16)
    repeated = jnp.repeat(tokens, top_count, axis=0)
    outgoing = jnp.dot(placing, repeated, preferred_element_type=jnp.float32).astype(jnp.bfloat16)
    outgoing = outgoing.reshape(experts, cap_slots, model_width)
    gate_rows = w_gate[0]
    up_rows = w_up[0]
    columns = gate_rows.shape[0]
    arrived = lax.all_to_all(outgoing, "expert", split_axis=0, concat_axis=0, tiled=True)
    local_hidden = hidden_block(
        lax.all_gather(arrived.reshape(-1, model_width), "fsdp", axis=0, tiled=True),
        gate_rows,
        up_rows,
    )
    shaped = local_hidden.reshape(fsdp_size, experts, cap_slots, columns)
    step_one = lax.all_to_all(shaped, "expert", split_axis=1, concat_axis=1, tiled=True)
    returned = lax.all_to_all(step_one, "fsdp", split_axis=0, concat_axis=3, tiled=True)
    returned = returned.reshape(experts * cap_slots, -1)
    collected = lax.dot_general(
        placing, returned, (((0,), (0,)), ((), ())), preferred_element_type=jnp.float32
    )
    routed = (router_weight.reshape(-1, 1) * collected).astype(jnp.bfloat16)
    return routed.reshape(tok_rows, top_count, -1)


def solution(mesh):
    return jax.shard_map(
        local,
        mesh=mesh,
        in_specs=(
            P(("expert", "fsdp"), None),
            P(("expert", "fsdp"), None),
            P(("expert", "fsdp"), None),
            P("expert", "fsdp", None),
            P("expert", "fsdp", None),
        ),
        out_specs=P(("expert", "fsdp"), None, None),
        check_vma=False,
    )
```

profile of v0, /device:TPU:1, one launch (start us, length us, event | category | flops | bytes accessed | tf_op | source)
XLA Modules:
  0.0 259.9 jit_solution(14394430911966610535)
XLA Ops:
  6.5 0.0 all-gather.2.cloned.1.call-start
  6.5 0.8 copy.13
  7.3 0.1 reshape.33
  7.4 0.1 fusion.20
  7.5 0.1 reduce_window_sum.11
  7.6 0.2 select_reduce_fusion
  7.8 1.2 broadcast_in_dim.2
  9.0 0.2 reshape.34
  9.2 0.4 convolution_convert_fusion
  9.6 0.5 reshape.35
  10.1 49.6 %all_to_all.25 = bf16[16,5,6144]{2,1,0:T(8,128)(2,1)S(1)} all-to-all(bf16[16,5,6144]{2,1,0:T(8,128)(2,1)S(1)} %reshape.35), channel_id=1, replica_groups=mesh['expert'=16,'fsdp'=16] {'expert'}, dimensions={0} | all-to-all | bytes 1966080 | tf_op jit(solution)/shard_map/all_to_all | solution.py:38
  59.6 1.2 reshape.36
  60.9 0.0 all-gather.2.cloned.1.call-update
  60.9 107.8 %all-gather.2.cloned.1.call-done = bf16[1280,6144]{1,0:T(8,128)(2,1)} async-done(((bf16[80,6144]{1,0:T(8,128)(2,1)}), bf16[1280,6144]{1,0:T(8,128)(2,1)}) %all-gather.2.cloned.1.call-update) | async-done | bytes 15728656 | tf_op jit(solution)/shard_map/all_gather | solution.py:40
  168.7 0.0 copy-start.1
  168.7 0.0 copy-start.2
  168.7 11.7 %fusion.3 = f32[1280,336]{0,1:T(8,128)S(1)} fusion(bf16[1280,6144]{1,0:T(8,128)(2,1)} %all-gather.2.cloned.1.call-done, bf16[1,336,6144]{2,1,0:T(8,128)(2,1)} %param.8), kind=kOutput, calls=%fused_computation.5 | convolution fusion | flops 5284823040 | bytes 21577728 | tf_op jit(solution)/shard_map/dot_general | solution.py:8
  180.5 0.0 copy-done.1
  180.5 0.5 copy-done.2
  181.0 8.9 %fusion.8 = bf16[1280,336]{0,1:T(8,128)(2,1)S(1)} fusion(bf16[1280,6144]{1,0:T(8,128)(2,1)S(1)} %copy-done.1, bf16[1,336,6144]{2,1,0:T(8,128)(2,1)S(1)} %copy-done.2, f32[1280,336]{0,1:T(8,128)S(1)} %fusion.3), kind=kOutput, calls=%fused_computation.8 | convolution fusion | flops 5313208320 | bytes 22437888 | tf_op jit(solution)/shard_map/dot_general | solution.py:11
  190.0 0.6 copy.14
  190.6 0.7 reshape.37
  191.3 0.7 copy.15
  192.0 34.7 %all_to_all.26 = bf16[16,16,5,336]{3,0,2,1:T(8,128)(2,1)S(1)} all-to-all(bf16[16,16,5,336]{3,0,2,1:T(8,128)(2,1)S(1)} %copy.15), channel_id=1, replica_groups=mesh['expert'=16,'fsdp'=16] {'expert'}, dimensions={1} | all-to-all | bytes 1720320 | tf_op jit(solution)/shard_map/all_to_all | solution.py:45
  226.7 0.0 copy-start
  226.7 1.2 copy.16
  227.8 5.0 %all-to-all-start.2 = ((bf16[16,16,5,336]{3,1,2,0:T(8,128)(2,1)}), bf16[16,16,5,336]{3,1,2,0:T(8,128)(2,1)S(1)}, u32[]{:S(2)}, u32[]{:S(2)}) async-start(bf16[16,16,5,336]{3,1,2,0:T(8,128)(2,1)} %copy.16), calls=%async_computation.2 | async-start | bytes 1966080 | tf_op jit(solution)/shard_map/all_to_all | solution.py:46
  232.8 0.0 copy-done
  232.8 0.1 copy.12
  232.9 0.1 mul.41
  233.0 17.3 %all-to-all-done.2 = bf16[16,16,5,336]{3,1,2,0:T(8,128)(2,1)S(1)} async-done(((bf16[16,16,5,336]{3,1,2,0:T(8,128)(2,1)}), bf16[16,16,5,336]{3,1,2,0:T(8,128)(2,1)S(1)}, u32[]{:S(2)}, u32[]{:S(2)}) %all-to-all-start.2) | async-done | bytes 860192 | tf_op jit(solution)/shard_map/all_to_all | solution.py:46
  250.3 0.2 copy.17
  250.5 1.2 reshape.38
  251.7 0.4 fusion
  252.1 1.0 reshape.39
  (1 shorter events, 0.0 us)
Async XLA Ops:
  6.5 162.2 %all-gather.2.cloned.1.call-start = ((), (), s32[]{:S(2)}) async-start(), calls=%async_computation.3 | async-start | bytes 16711680 | tf_op jit(solution)/shard_map/all_gather | solution.py:40
  168.7 11.8 %copy-start.1 = (bf16[1280,6144]{1,0:T(8,128)(2,1)S(1)}, bf16[1280,6144]{1,0:T(8,128)(2,1)}, u32[]{:S(2)}) copy-start(bf16[1280,6144]{1,0:T(8,128)(2,1)} %all-gather.2.cloned.1.call-done) | copy-start | bytes 47185924
  168.7 12.3 %copy-start.2 = (bf16[1,336,6144]{2,1,0:T(8,128)(2,1)S(1)}, bf16[1,336,6144]{2,1,0:T(8,128)(2,1)}, u32[]{:S(2)}) copy-start(bf16[1,336,6144]{2,1,0:T(8,128)(2,1)} %param.9) | copy-start | bytes 12386308
  226.7 6.2 %copy-start = (f32[16,4]{0,1:T(4,128)S(1)}, f32[16,4]{0,1:T(4,128)}, u32[]{:S(2)}) copy-start(f32[16,4]{0,1:T(4,128)} %param.7) | copy-start | bytes 772
  227.8 22.5 %all-to-all-start.2 = ((bf16[16,16,5,336]{3,1,2,0:T(8,128)(2,1)}), bf16[16,16,5,336]{3,1,2,0:T(8,128)(2,1)S(1)}, u32[]{:S(2)}, u32[]{:S(2)}) async-start(bf16[16,16,5,336]{3,1,2,0:T(8,128)(2,1)} %copy.16), calls=%async_computation.2 | async-start | bytes 1966080 | tf_op jit(solution)/shard_map/all_to_all | solution.py:46
Sparse Core Ops, SparseCore 0:
  61.0 107.6 all-gather.1
where the time goes:
time: 260 us
  waiting for transfers between devices  125 us (48%)
  blocking collectives  84.3 us (32%)
  matrix products  21.5 us (8%)
  between operations  13.5 us (5%)
  local copies, waits for them, and re-layouts  10.2 us (4%)
  starting transfers between devices  4.97 us (2%)
    all_gather x1, waiting for transfers between devices, local(): lax.all_gather(arrived.reshape(-1, model_width), 'fsdp', axis=0, tiled=True)  108 us
    all_to_all x1, blocking collectives, local(): lax.all_to_all(outgoing, 'expert', split_axis=0, concat_axis=0, tiled=True)  49.6 us
    all_to_all x1, blocking collectives, local(): lax.all_to_all(shaped, 'expert', split_axis=1, concat_axis=1, tiled=True)  34.7 us
    all_to_all x1, waiting for transfers between devices, local(): lax.all_to_all(step_one, 'fsdp', split_axis=0, concat_axis=3, tiled=True)  17.3 us
    dot_general x1, matrix products, hidden_block(): lax.dot_general(row_block, gate_rows, (((1,), (1,)), ((), ())), preferred...  11.7 us
    dot_general x1, matrix products, hidden_block(): lax.dot_general(row_block, up_rows, (((1,), (1,)), ((), ())), preferred_e...  8.93 us
  transfers between devices with their start and end apart: 2, of which 2 were waited for; matrix products, arithmetic and copies ran while one was open for 0% of the time, Pallas kernels for 0%

commit v1 on v0

--- a/solution.py
+++ b/solution.py
@@ -42,9 +42,10 @@
         up_rows,
     )
     shaped = local_hidden.reshape(fsdp_size, experts, cap_slots, columns)
-    step_one = lax.all_to_all(shaped, "expert", split_axis=1, concat_axis=1, tiled=True)
-    returned = lax.all_to_all(step_one, "fsdp", split_axis=0, concat_axis=3, tiled=True)
-    returned = returned.reshape(experts * cap_slots, -1)
+    by_owner = jnp.transpose(shaped, (1, 0, 2, 3)).reshape(experts * fsdp_size, cap_slots, columns)
+    returned = lax.all_to_all(by_owner, ("expert", "fsdp"), 0, 0, tiled=True)
+    returned = returned.reshape(experts, fsdp_size, cap_slots, columns)
+    returned = jnp.transpose(returned, (0, 2, 1, 3)).reshape(experts * cap_slots, -1)
     collected = lax.dot_general(
         placing, returned, (((0,), (0,)), ((), ())), preferred_element_type=jnp.float32
     )

time: 260 us -> 256 us (0.985)
  blocking collectives: 84.3 us -> 49.6 us
  waiting for transfers between devices: 125 us -> 149 us
  starting transfers between devices: 4.97 us -> 11.6 us
    all_to_all x1 -> x0, blocking collectives: 34.7 us -> none  [local(): lax.all_to_all(shaped, 'expert', split_axis=1, concat_axis=1, tiled=True)]
    all_to_all x1, waiting for transfers between devices: 17.3 us -> 40.8 us  [local(): returned = lax.all_to_all(by_owner, ('expert', 'fsdp'), 0, 0, tiled=True)]
    all_to_all x1, starting transfers between devices: 4.97 us -> 11.6 us  [local(): returned = lax.all_to_all(by_owner, ('expert', 'fsdp'), 0, 0, tiled=True)]
where the time goes in v1:
time: 256 us
  waiting for transfers between devices  149 us (58%)
  blocking collectives  49.6 us (19%)
  matrix products  21.5 us (8%)
  between operations  13.5 us (5%)
  starting transfers between devices  11.6 us (5%)
  local copies, waits for them, and re-layouts  10.8 us (4%)
    all_gather x1, waiting for transfers between devices, local(): lax.all_gather(arrived.reshape(-1, model_width), 'fsdp', axis=0, tiled=True)  108 us
    all_to_all x1, blocking collectives, local(): lax.all_to_all(outgoing, 'expert', split_axis=0, concat_axis=0, tiled=True)  49.6 us
    all_to_all x1, waiting for transfers between devices, local(): returned = lax.all_to_all(by_owner, ('expert', 'fsdp'), 0, 0, tiled=True)  40.8 us
    dot_general x1, matrix products, hidden_block(): lax.dot_general(row_block, gate_rows, (((1,), (1,)), ((), ())), preferred...  11.7 us
    all_to_all x1, starting transfers between devices, local(): returned = lax.all_to_all(by_owner, ('expert', 'fsdp'), 0, 0, tiled=True)  11.6 us
    dot_general x1, matrix products, hidden_block(): lax.dot_general(row_block, up_rows, (((1,), (1,)), ((), ())), preferred_e...  8.93 us
  transfers between devices with their start and end apart: 2, of which 2 were waited for; matrix products, arithmetic and copies ran while one was open for 0% of the time, Pallas kernels for 0%

profile of v1, /device:TPU:1, one launch (start us, length us, event | category | flops | bytes accessed | tf_op | source)
XLA Modules:
  0.0 256.0 jit_solution(8228887948077420177)
XLA Ops:
  6.5 0.0 all-gather.2.cloned.1.call-start
  6.5 0.8 copy.14
  7.3 0.1 reshape.38
  7.4 0.1 fusion.20
  7.5 0.1 reduce_window_sum.11
  7.6 0.2 select_reduce_fusion
  7.8 1.2 broadcast_in_dim.2
  9.0 0.2 reshape.39
  9.2 0.4 convolution_convert_fusion
  9.6 0.5 reshape.40
  10.1 49.6 %all_to_all.10 = bf16[16,5,6144]{2,1,0:T(8,128)(2,1)S(1)} all-to-all(bf16[16,5,6144]{2,1,0:T(8,128)(2,1)S(1)} %reshape.40), channel_id=1, replica_groups=mesh['expert'=16,'fsdp'=16] {'expert'}, dimensions={0} | all-to-all | bytes 1966080 | tf_op jit(solution)/shard_map/all_to_all | solution.py:38
  59.6 1.2 reshape.41
  60.9 0.0 all-gather.2.cloned.1.call-update
  60.9 107.8 %all-gather.2.cloned.1.call-done = bf16[1280,6144]{1,0:T(8,128)(2,1)} async-done(((bf16[80,6144]{1,0:T(8,128)(2,1)}), bf16[1280,6144]{1,0:T(8,128)(2,1)}) %all-gather.2.cloned.1.call-update) | async-done | bytes 15728656 | tf_op jit(solution)/shard_map/all_gather | solution.py:40
  168.7 0.0 copy-start.1
  168.7 0.0 copy-start.2
  168.7 11.7 %fusion.3 = f32[1280,336]{0,1:T(8,128)S(1)} fusion(bf16[1280,6144]{1,0:T(8,128)(2,1)} %all-gather.2.cloned.1.call-done, bf16[1,336,6144]{2,1,0:T(8,128)(2,1)} %param.8), kind=kOutput, calls=%fused_computation.5 | convolution fusion | flops 5284823040 | bytes 21577728 | tf_op jit(solution)/shard_map/dot_general | solution.py:8
  180.5 0.0 copy-done.1
  180.5 0.5 copy-done.2
  181.0 8.9 %fusion.8 = bf16[1280,336]{0,1:T(8,128)(2,1)S(1)} fusion(bf16[1280,6144]{1,0:T(8,128)(2,1)S(1)} %copy-done.1, bf16[1,336,6144]{2,1,0:T(8,128)(2,1)S(1)} %copy-done.2, f32[1280,336]{0,1:T(8,128)S(1)} %fusion.3), kind=kOutput, calls=%fused_computation.8 | convolution fusion | flops 5313208320 | bytes 22437888 | tf_op jit(solution)/shard_map/dot_general | solution.py:11
  190.0 0.6 copy.15
  190.6 0.7 reshape.42
  191.3 0.7 copy.16
  192.0 1.8 copy.17
  193.8 0.0 copy-start
  193.8 11.6 %all-to-all-start.1 = ((bf16[256,5,336]{2,1,0:T(8,128)(2,1)}), bf16[256,5,336]{2,1,0:T(8,128)(2,1)S(1)}, u32[]{:S(2)}, u32[]{:S(2)}) async-start(bf16[256,5,336]{2,1,0:T(8,128)(2,1)} %copy.17), calls=%async_computation.1 | async-start | bytes 3145728 | tf_op jit(solution)/shard_map/all_to_all | solution.py:46
  205.4 0.0 copy-done
  205.4 0.1 copy.13
  205.5 0.1 mul.41
  205.6 40.8 %all-to-all-done.1 = bf16[256,5,336]{2,1,0:T(8,128)(2,1)S(1)} async-done(((bf16[256,5,336]{2,1,0:T(8,128)(2,1)}), bf16[256,5,336]{2,1,0:T(8,128)(2,1)S(1)}, u32[]{:S(2)}, u32[]{:S(2)}) %all-to-all-start.1) | async-done | bytes 860192 | tf_op jit(solution)/shard_map/all_to_all | solution.py:46
  246.4 0.1 copy.20
  246.6 1.2 reshape.45
  247.7 0.4 fusion
  248.1 1.0 reshape.46
  (1 shorter events, 0.0 us)
Async XLA Ops:
  6.5 162.2 %all-gather.2.cloned.1.call-start = ((), (), s32[]{:S(2)}) async-start(), calls=%async_computation.2 | async-start | bytes 16711680 | tf_op jit(solution)/shard_map/all_gather | solution.py:40
  168.7 11.8 %copy-start.1 = (bf16[1280,6144]{1,0:T(8,128)(2,1)S(1)}, bf16[1280,6144]{1,0:T(8,128)(2,1)}, u32[]{:S(2)}) copy-start(bf16[1280,6144]{1,0:T(8,128)(2,1)} %all-gather.2.cloned.1.call-done) | copy-start | bytes 47185924
  168.7 12.3 %copy-start.2 = (bf16[1,336,6144]{2,1,0:T(8,128)(2,1)S(1)}, bf16[1,336,6144]{2,1,0:T(8,128)(2,1)}, u32[]{:S(2)}) copy-start(bf16[1,336,6144]{2,1,0:T(8,128)(2,1)} %param.9) | copy-start | bytes 12386308
  193.8 11.6 %copy-start = (f32[16,4]{0,1:T(4,128)S(1)}, f32[16,4]{0,1:T(4,128)}, u32[]{:S(2)}) copy-start(f32[16,4]{0,1:T(4,128)} %param.7) | copy-start | bytes 772
  193.8 52.6 %all-to-all-start.1 = ((bf16[256,5,336]{2,1,0:T(8,128)(2,1)}), bf16[256,5,336]{2,1,0:T(8,128)(2,1)S(1)}, u32[]{:S(2)}, u32[]{:S(2)}) async-start(bf16[256,5,336]{2,1,0:T(8,128)(2,1)} %copy.17), calls=%async_computation.1 | async-start | bytes 3145728 | tf_op jit(solution)/shard_map/all_to_all | solution.py:46
Sparse Core Ops, SparseCore 0:
  61.0 107.6 all-gather.1

commit v2 on v1

--- a/solution.py
+++ b/solution.py
@@ -35,14 +35,16 @@
     gate_rows = w_gate[0]
     up_rows = w_up[0]
     columns = gate_rows.shape[0]
-    arrived = lax.all_to_all(outgoing, "expert", split_axis=0, concat_axis=0, tiled=True)
+    block = cap_slots * model_width
+    dense = outgoing.reshape(experts, block // 128, 128)
+    arrived = lax.all_to_all(dense, "expert", split_axis=0, concat_axis=0, tiled=True)
     local_hidden = hidden_block(
         lax.all_gather(arrived.reshape(-1, model_width), "fsdp", axis=0, tiled=True),
         gate_rows,
         up_rows,
     )
     shaped = local_hidden.reshape(fsdp_size, experts, cap_slots, columns)
-    by_owner = jnp.transpose(shaped, (1, 0, 2, 3)).reshape(experts * fsdp_size, cap_slots, columns)
+    by_owner = jnp.transpose(shaped, (1, 0, 2, 3)).reshape(experts * fsdp_size, 16, -1)
     returned = lax.all_to_all(by_owner, ("expert", "fsdp"), 0, 0, tiled=True)
     returned = returned.reshape(experts, fsdp_size, cap_slots, columns)
     returned = jnp.transpose(returned, (0, 2, 1, 3)).reshape(experts * cap_slots, -1)

time: 256 us -> 237 us (0.926)
  blocking collectives: 49.6 us -> 36.9 us
  waiting for transfers between devices: 149 us -> 138 us
  local copies, waits for them, and re-layouts: 10.8 us -> 14.5 us
    all_to_all x1, blocking collectives: 49.6 us -> 36.9 us  [local(): lax.all_to_all(dense, 'expert', split_axis=0, concat_axis=0, tiled=True)]
    all_to_all x1, waiting for transfers between devices: 40.8 us -> 30.2 us  [local(): returned = lax.all_to_all(by_owner, ('expert', 'fsdp'), 0, 0, tiled=True)]
where the time goes in v2:
time: 237 us; the launch traced here: 236 us
  waiting for transfers between devices  138 us (58%)
  blocking collectives  36.9 us (16%)
  matrix products  21.5 us (9%)
  local copies, waits for them, and re-layouts  14.5 us (6%)
  between operations  13.5 us (6%)
  starting transfers between devices  11.6 us (5%)
    all_gather x1, waiting for transfers between devices, local(): lax.all_gather(arrived.reshape(-1, model_width), 'fsdp', axis=0, tiled=True)  108 us
    all_to_all x1, blocking collectives, local(): lax.all_to_all(dense, 'expert', split_axis=0, concat_axis=0, tiled=True)  36.9 us
    all_to_all x1, waiting for transfers between devices, local(): returned = lax.all_to_all(by_owner, ('expert', 'fsdp'), 0, 0, tiled=True)  30.2 us
    dot_general x1, matrix products, hidden_block(): lax.dot_general(row_block, gate_rows, (((1,), (1,)), ((), ())), preferred...  11.7 us
    all_to_all x1, starting transfers between devices, local(): returned = lax.all_to_all(by_owner, ('expert', 'fsdp'), 0, 0, tiled=True)  11.6 us
    dot_general x1, matrix products, hidden_block(): lax.dot_general(row_block, up_rows, (((1,), (1,)), ((), ())), preferred_e...  8.94 us
  transfers between devices with their start and end apart: 2, of which 2 were waited for; matrix products, arithmetic and copies ran while one was open for 0% of the time, Pallas kernels for 0%

profile of v2, /device:TPU:1, one launch (start us, length us, event | category | flops | bytes accessed | tf_op | source)
XLA Modules:
  0.0 236.4 jit_solution(7650815113321922271)
XLA Ops:
  6.5 0.0 all-gather.2.cloned.1.call-start
  6.5 0.8 copy.9
  7.3 0.1 reshape.35
  7.4 0.1 fusion.20
  7.5 0.1 reduce_window_sum.11
  7.6 0.2 select_reduce_fusion
  7.8 1.2 broadcast_in_dim.2
  9.0 0.2 reshape.36
  9.2 0.4 convolution_convert_fusion
  9.6 0.4 reshape_reshape.3
  10.0 36.9 %all_to_all.10 = bf16[16,240,128]{2,1,0:T(8,128)(2,1)S(1)} all-to-all(bf16[16,240,128]{2,1,0:T(8,128)(2,1)S(1)} %reshape_reshape.3), channel_id=1, replica_groups=mesh['expert'=16,'fsdp'=16] {'expert'}, dimensions={0} | all-to-all | bytes 1966080 | tf_op jit(solution)/shard_map/all_to_all | solution.py:40
  47.0 1.4 reshape.37
  48.4 0.0 all-gather.2.cloned.1.call-update
  48.4 107.8 %all-gather.2.cloned.1.call-done = bf16[1280,6144]{1,0:T(8,128)(2,1)} async-done(((bf16[80,6144]{1,0:T(8,128)(2,1)}), bf16[1280,6144]{1,0:T(8,128)(2,1)}) %all-gather.2.cloned.1.call-update) | async-done | bytes 15728656 | tf_op jit(solution)/shard_map/all_gather | solution.py:42
  156.2 0.0 copy-start.1
  156.2 0.0 copy-start.2
  156.2 11.7 %fusion.3 = f32[1280,336]{0,1:T(8,128)S(1)} fusion(bf16[1280,6144]{1,0:T(8,128)(2,1)} %all-gather.2.cloned.1.call-done, bf16[1,336,6144]{2,1,0:T(8,128)(2,1)} %param.8), kind=kOutput, calls=%fused_computation.5 | convolution fusion | flops 5284823040 | bytes 21577728 | tf_op jit(solution)/shard_map/dot_general | solution.py:8
  168.0 0.0 copy-done.1
  168.0 0.5 copy-done.2
  168.5 8.9 %fusion.8 = bf16[1280,336]{0,1:T(8,128)(2,1)S(1)} fusion(bf16[1280,6144]{1,0:T(8,128)(2,1)S(1)} %copy-done.1, bf16[1,336,6144]{2,1,0:T(8,128)(2,1)S(1)} %copy-done.2, f32[1280,336]{0,1:T(8,128)S(1)} %fusion.3), kind=kOutput, calls=%fused_computation.8 | convolution fusion | flops 5313208320 | bytes 22437888 | tf_op jit(solution)/shard_map/dot_general | solution.py:11
  177.4 0.6 copy.10
  178.1 0.7 reshape.38
  178.8 0.2 copy.11
  179.0 0.0 copy-start
  179.0 3.3 %reshape.39 = bf16[256,16,105]{2,1,0:T(8,128)(2,1)} reshape(bf16[16,16,5,336]{3,2,1,0:T(8,128)(2,1)S(1)} %copy.11) | data formatting | bytes 1720320 | tf_op jit(solution)/shard_map/reshape | solution.py:47
  182.4 11.6 %all-to-all-start.1 = ((bf16[256,16,105]{2,1,0:T(8,128)(2,1)}), bf16[256,16,105]{2,1,0:T(8,128)(2,1)S(1)}, u32[]{:S(2)}, u32[]{:S(2)}) async-start(bf16[256,16,105]{2,1,0:T(8,128)(2,1)} %reshape.39), calls=%async_computation.1 | async-start | bytes 2097152 | tf_op jit(solution)/shard_map/all_to_all | solution.py:48
  194.0 0.0 copy-done
  194.0 0.1 copy.8
  194.1 0.1 mul.41
  194.2 30.2 %all-to-all-done.1 = bf16[256,16,105]{2,1,0:T(8,128)(2,1)S(1)} async-done(((bf16[256,16,105]{2,1,0:T(8,128)(2,1)}), bf16[256,16,105]{2,1,0:T(8,128)(2,1)S(1)}, u32[]{:S(2)}, u32[]{:S(2)}) %all-to-all-start.1) | async-done | bytes 860192 | tf_op jit(solution)/shard_map/all_to_all | solution.py:48
  224.3 2.5 %reshape.40 = bf16[16,16,5,336]{3,2,1,0:T(8,128)(2,1)S(1)} reshape(bf16[256,16,105]{2,1,0:T(8,128)(2,1)S(1)} %all-to-all-done.1) | data formatting | bytes 1720320 | tf_op jit(solution)/shard_map/reshape | solution.py:49
  226.9 0.1 copy.12
  227.0 1.2 reshape.41
  228.2 0.4 fusion
  228.6 1.0 reshape.42
  (1 shorter events, 0.0 us)
Async XLA Ops:
  6.5 149.7 %all-gather.2.cloned.1.call-start = ((), (), s32[]{:S(2)}) async-start(), calls=%async_computation.2 | async-start | bytes 16711680 | tf_op jit(solution)/shard_map/all_gather | solution.py:42
  156.2 11.8 %copy-start.1 = (bf16[1280,6144]{1,0:T(8,128)(2,1)S(1)}, bf16[1280,6144]{1,0:T(8,128)(2,1)}, u32[]{:S(2)}) copy-start(bf16[1280,6144]{1,0:T(8,128)(2,1)} %all-gather.2.cloned.1.call-done) | copy-start | bytes 47185924
  156.2 12.3 %copy-start.2 = (bf16[1,336,6144]{2,1,0:T(8,128)(2,1)S(1)}, bf16[1,336,6144]{2,1,0:T(8,128)(2,1)}, u32[]{:S(2)}) copy-start(bf16[1,336,6144]{2,1,0:T(8,128)(2,1)} %param.9) | copy-start | bytes 12386308
  179.0 15.0 %copy-start = (f32[16,4]{0,1:T(4,128)S(1)}, f32[16,4]{0,1:T(4,128)}, u32[]{:S(2)}) copy-start(f32[16,4]{0,1:T(4,128)} %param.7) | copy-start | bytes 772
  182.4 42.0 %all-to-all-start.1 = ((bf16[256,16,105]{2,1,0:T(8,128)(2,1)}), bf16[256,16,105]{2,1,0:T(8,128)(2,1)S(1)}, u32[]{:S(2)}, u32[]{:S(2)}) async-start(bf16[256,16,105]{2,1,0:T(8,128)(2,1)} %reshape.39), calls=%async_computation.1 | async-start | bytes 2097152 | tf_op jit(solution)/shard_map/all_to_all | solution.py:48
Sparse Core Ops, SparseCore 0:
  48.5 107.6 all-gather.1

commit v3 on v2

--- a/solution.py
+++ b/solution.py
@@ -5,12 +5,13 @@
 
 
 def hidden_block(row_block, gate_rows, up_rows):
-    gate_act = lax.dot_general(
-        row_block, gate_rows, (((1,), (1,)), ((), ())), preferred_element_type=jnp.float32
+    columns = gate_rows.shape[0]
+    both = jnp.concatenate([gate_rows, up_rows], axis=0)
+    acts = lax.dot_general(
+        row_block, both, (((1,), (1,)), ((), ())), preferred_element_type=jnp.float32
     )
-    up_act = lax.dot_general(
-        row_block, up_rows, (((1,), (1,)), ((), ())), preferred_element_type=jnp.float32
-    )
+    gate_act = acts[:, :columns]
+    up_act = acts[:, columns:]
     return (jax.nn.gelu(gate_act, approximate=False) * up_act).astype(jnp.bfloat16)
 
 

time: 237 us -> 235 us (level)
  matrix products: 21.5 us -> 16.3 us
  other arithmetic: 0.36 us -> 4.14 us
    dot_general x2 -> x1, matrix products: 20.7 us -> 15.5 us  [hidden_block(): lax.dot_general(row_block, both, (((1,), (1,)), ((), ())), preferred_elem...]
    convert_element_type x0 -> x1, other arithmetic: none -> 3.79 us  [hidden_block(): (jax.nn.gelu(gate_act, approximate=False) * up_act).astype(jnp.bfloat16)]
where the time goes in v3:
time: 235 us; the launch traced here: 234 us
  waiting for transfers between devices  138 us (59%)
  blocking collectives  36.9 us (16%)
  matrix products  16.3 us (7%)
  local copies, waits for them, and re-layouts  13.8 us (6%)
  between operations  13.5 us (6%)
  starting transfers between devices  11.6 us (5%)
  other arithmetic  4.14 us (2%)
    all_gather x1, waiting for transfers between devices, local(): lax.all_gather(arrived.reshape(-1, model_width), 'fsdp', axis=0, tiled=True)  108 us
    all_to_all x1, blocking collectives, local(): lax.all_to_all(dense, 'expert', split_axis=0, concat_axis=0, tiled=True)  36.9 us
    all_to_all x1, waiting for transfers between devices, local(): returned = lax.all_to_all(by_owner, ('expert', 'fsdp'), 0, 0, tiled=True)  30.1 us
    dot_general x1, matrix products, hidden_block(): lax.dot_general(row_block, both, (((1,), (1,)), ((), ())), preferred_elem...  15.5 us
    all_to_all x1, starting transfers between devices, local(): returned = lax.all_to_all(by_owner, ('expert', 'fsdp'), 0, 0, tiled=True)  11.6 us
  transfers between devices with their start and end apart: 2, of which 2 were waited for; matrix products, arithmetic and copies ran while one was open for 0% of the time, Pallas kernels for 0%

profile of v3, /device:TPU:1, one launch (start us, length us, event | category | flops | bytes accessed | tf_op | source)
XLA Modules:
  0.0 234.4 jit_solution(17881764356394677500)
XLA Ops:
  6.5 0.0 all-gather.2.cloned.1.call-start
  6.5 0.8 copy.9
  7.3 0.1 reshape.35
  7.4 0.1 fusion.16
  7.5 0.1 reduce_window_sum.11
  7.6 0.2 select_reduce_fusion
  7.8 1.2 broadcast_in_dim.2
  9.0 0.2 reshape.36
  9.2 0.4 convolution_convert_fusion
  9.6 0.4 reshape_reshape.3
  10.0 36.9 %all_to_all.10 = bf16[16,240,128]{2,1,0:T(8,128)(2,1)S(1)} all-to-all(bf16[16,240,128]{2,1,0:T(8,128)(2,1)S(1)} %reshape_reshape.3), channel_id=1, replica_groups=mesh['expert'=16,'fsdp'=16] {'expert'}, dimensions={0} | all-to-all | bytes 1966080 | tf_op jit(solution)/shard_map/all_to_all | solution.py:41
  47.0 1.4 reshape.37
  48.4 0.0 all-gather.2.cloned.1.call-update
  48.4 107.8 %all-gather.2.cloned.1.call-done = bf16[1280,6144]{1,0:T(8,128)(2,1)} async-done(((bf16[80,6144]{1,0:T(8,128)(2,1)}), bf16[1280,6144]{1,0:T(8,128)(2,1)}) %all-gather.2.cloned.1.call-update) | async-done | bytes 15728656 | tf_op jit(solution)/shard_map/all_gather | solution.py:43
  156.2 15.5 %fusion = f32[1280,672]{0,1:T(8,128)S(1)} fusion(bf16[1280,6144]{1,0:T(8,128)(2,1)} %all-gather.2.cloned.1.call-done, bf16[336,6144]{1,0:T(8,128)(2,1)} %bitcast.11, bf16[336,6144]{1,0:T(8,128)(2,1)} %bitcast.12), kind=kOutput, calls=%fused_computation | convolution fusion | flops 10586161152 | bytes 27426816 | tf_op jit(solution)/shard_map/dot_general | solution.py:10
  171.7 3.8 %fusion.8 = bf16[1280,336]{0,1:T(8,128)(2,1)S(1)} fusion(f32[1280,672]{0,1:T(8,128)S(1)} %fusion), kind=kLoop, calls=%fused_computation.11 | loop fusion | flops 28385280 | bytes 4300800 | tf_op jit(solution)/shard_map/convert_element_type | solution.py:15
  175.5 0.6 copy.10
  176.2 0.5 reshape.38
  176.7 0.2 copy.11
  176.9 0.0 copy-start
  176.9 3.4 %reshape.39 = bf16[256,16,105]{2,1,0:T(8,128)(2,1)} reshape(bf16[16,16,5,336]{3,2,1,0:T(8,128)(2,1)S(1)} %copy.11) | data formatting | bytes 1720320 | tf_op jit(solution)/shard_map/reshape | solution.py:48
  180.3 11.6 %all-to-all-start.1 = ((bf16[256,16,105]{2,1,0:T(8,128)(2,1)}), bf16[256,16,105]{2,1,0:T(8,128)(2,1)S(1)}, u32[]{:S(2)}, u32[]{:S(2)}) async-start(bf16[256,16,105]{2,1,0:T(8,128)(2,1)} %reshape.39), calls=%async_computation.1 | async-start | bytes 2097152 | tf_op jit(solution)/shard_map/all_to_all | solution.py:49
  191.9 0.0 copy-done
  192.0 0.1 copy.8
  192.0 0.1 mul.41
  192.1 30.1 %all-to-all-done.1 = bf16[256,16,105]{2,1,0:T(8,128)(2,1)S(1)} async-done(((bf16[256,16,105]{2,1,0:T(8,128)(2,1)}), bf16[256,16,105]{2,1,0:T(8,128)(2,1)S(1)}, u32[]{:S(2)}, u32[]{:S(2)}) %all-to-all-start.1) | async-done | bytes 860192 | tf_op jit(solution)/shard_map/all_to_all | solution.py:49
  222.3 2.5 %reshape.40 = bf16[16,16,5,336]{3,2,1,0:T(8,128)(2,1)S(1)} reshape(bf16[256,16,105]{2,1,0:T(8,128)(2,1)S(1)} %all-to-all-done.1) | data formatting | bytes 1720320 | tf_op jit(solution)/shard_map/reshape | solution.py:50
  224.8 0.1 copy.12
  225.0 1.2 reshape.41
  226.1 0.4 fusion.4
  226.5 1.0 reshape.42
  (1 shorter events, 0.0 us)
Async XLA Ops:
  6.5 149.7 %all-gather.2.cloned.1.call-start = ((), (), s32[]{:S(2)}) async-start(), calls=%async_computation.2 | async-start | bytes 16711680 | tf_op jit(solution)/shard_map/all_gather | solution.py:43
  176.9 15.0 %copy-start = (f32[16,4]{0,1:T(4,128)S(1)}, f32[16,4]{0,1:T(4,128)}, u32[]{:S(2)}) copy-start(f32[16,4]{0,1:T(4,128)} %param.7) | copy-start | bytes 772
  180.3 42.0 %all-to-all-start.1 = ((bf16[256,16,105]{2,1,0:T(8,128)(2,1)}), bf16[256,16,105]{2,1,0:T(8,128)(2,1)S(1)}, u32[]{:S(2)}, u32[]{:S(2)}) async-start(bf16[256,16,105]{2,1,0:T(8,128)(2,1)} %reshape.39), calls=%async_computation.1 | async-start | bytes 2097152 | tf_op jit(solution)/shard_map/all_to_all | solution.py:49
Sparse Core Ops, SparseCore 0:
  48.5 107.6 all-gather.1

commit v4 on v3

--- a/solution.py
+++ b/solution.py
@@ -27,11 +27,12 @@
     )
     slot_rank = jnp.sum((jnp.cumsum(choosing, axis=0) - 1) * choosing, axis=1)
     slot_of = flat_ids * cap_slots + slot_rank
-    placing = (
-        slot_of[None, :] == jnp.arange(experts * cap_slots, dtype=jnp.int32)[:, None]
+    slots = jnp.arange(experts * cap_slots, dtype=jnp.int32)
+    placing = (slot_of.reshape(tok_rows, top_count)[:, :, None] == slots).astype(jnp.bfloat16)
+    by_token = jnp.sum(placing, axis=1)
+    outgoing = lax.dot_general(
+        by_token, tokens, (((0,), (0,)), ((), ())), preferred_element_type=jnp.float32
     ).astype(jnp.bfloat16)
-    repeated = jnp.repeat(tokens, top_count, axis=0)
-    outgoing = jnp.dot(placing, repeated, preferred_element_type=jnp.float32).astype(jnp.bfloat16)
     outgoing = outgoing.reshape(experts, cap_slots, model_width)
     gate_rows = w_gate[0]
     up_rows = w_up[0]
@@ -50,10 +51,9 @@
     returned = returned.reshape(experts, fsdp_size, cap_slots, columns)
     returned = jnp.transpose(returned, (0, 2, 1, 3)).reshape(experts * cap_slots, -1)
     collected = lax.dot_general(
-        placing, returned, (((0,), (0,)), ((), ())), preferred_element_type=jnp.float32
+        placing, returned, (((2,), (0,)), ((), ())), preferred_element_type=jnp.float32
     )
-    routed = (router_weight.reshape(-1, 1) * collected).astype(jnp.bfloat16)
-    return routed.reshape(tok_rows, top_count, -1)
+    return (router_weight[:, :, None] * collected).astype(jnp.bfloat16)
 
 
 def solution(mesh):

time: 235 us -> 233 us (level)
  blocking collectives: 36.9 us -> 78.7 us
  waiting for transfers between devices: 138 us -> 108 us
  starting transfers between devices: 11.6 us -> 0.01 us
    all_to_all x0 -> x1, blocking collectives: none -> 41.8 us  [local(): returned = lax.all_to_all(by_owner, ('expert', 'fsdp'), 0, 0, tiled=True)]
    all_to_all x1 -> x0, waiting for transfers between devices: 30.1 us -> none  [local(): returned = lax.all_to_all(by_owner, ('expert', 'fsdp'), 0, 0, tiled=True)]
    all_to_all x1 -> x0, starting transfers between devices: 11.6 us -> none  [local(): returned = lax.all_to_all(by_owner, ('expert', 'fsdp'), 0, 0, tiled=True)]
  transfers between devices with their start and end apart: 2 -> 1, of which waited for: 2 -> 1; matrix products, arithmetic and copies ran while one was open for 0% -> 0% of each run, Pallas kernels for 0% -> 0%
where the time goes in v4:
time: 233 us
  waiting for transfers between devices  108 us (46%)
  blocking collectives  78.7 us (34%)
  matrix products  16.3 us (7%)
  between operations  13.5 us (6%)
  local copies, waits for them, and re-layouts  11.9 us (5%)
  other arithmetic  4.92 us (2%)
    all_gather x1, waiting for transfers between devices, local(): lax.all_gather(arrived.reshape(-1, model_width), 'fsdp', axis=0, tiled=True)  108 us
    all_to_all x1, blocking collectives, local(): returned = lax.all_to_all(by_owner, ('expert', 'fsdp'), 0, 0, tiled=True)  41.8 us
    all_to_all x1, blocking collectives, local(): lax.all_to_all(dense, 'expert', split_axis=0, concat_axis=0, tiled=True)  36.9 us
    dot_general x1, matrix products, hidden_block(): lax.dot_general(row_block, both, (((1,), (1,)), ((), ())), preferred_elem...  15.5 us
  transfers between devices with their start and end apart: 1, of which 1 were waited for; matrix products, arithmetic and copies ran while one was open for 0% of the time, Pallas kernels for 0%

profile of v4, /device:TPU:1, one launch (start us, length us, event | category | flops | bytes accessed | tf_op | source)
XLA Modules:
  0.0 233.2 jit_solution(7593001214646339488)
XLA Ops:
  6.5 0.0 copy-start
  6.5 0.0 all-gather.2.cloned.1.call-start
  6.5 0.8 copy.17
  7.3 0.1 eq.28
  7.4 0.1 fusion.17
  7.5 0.1 reduce_window_sum.11
  7.6 0.2 select_reduce_fusion
  7.8 0.1 reduce_sum.24
  7.9 0.1 copy.18
  8.0 0.7 multiply_add_fusion
  8.7 0.1 fusion.18
  8.7 0.0 copy-done
  8.8 0.4 convolution_convert_fusion
  9.2 0.4 reshape_reshape.3
  9.7 36.9 %all_to_all.10 = bf16[16,240,128]{2,1,0:T(8,128)(2,1)S(1)} all-to-all(bf16[16,240,128]{2,1,0:T(8,128)(2,1)S(1)} %reshape_reshape.3), channel_id=1, replica_groups=mesh['expert'=16,'fsdp'=16] {'expert'}, dimensions={0} | all-to-all | bytes 1966080 | tf_op jit(solution)/shard_map/all_to_all | solution.py:42
  46.6 1.4 reshape.24
  48.0 0.0 all-gather.2.cloned.1.call-update
  48.0 107.8 %all-gather.2.cloned.1.call-done = bf16[1280,6144]{1,0:T(8,128)(2,1)} async-done(((bf16[80,6144]{1,0:T(8,128)(2,1)}), bf16[1280,6144]{1,0:T(8,128)(2,1)}) %all-gather.2.cloned.1.call-update) | async-done | bytes 15728656 | tf_op jit(solution)/shard_map/all_gather | solution.py:44
  155.8 15.5 %fusion = f32[1280,672]{0,1:T(8,128)S(1)} fusion(bf16[1280,6144]{1,0:T(8,128)(2,1)} %all-gather.2.cloned.1.call-done, bf16[336,6144]{1,0:T(8,128)(2,1)} %bitcast.12, bf16[336,6144]{1,0:T(8,128)(2,1)} %bitcast.13), kind=kOutput, calls=%fused_computation | convolution fusion | flops 10586161152 | bytes 27426816 | tf_op jit(solution)/shard_map/dot_general | solution.py:10
  171.3 3.8 %fusion.8 = bf16[1280,336]{0,1:T(8,128)(2,1)S(1)} fusion(f32[1280,672]{0,1:T(8,128)S(1)} %fusion), kind=kLoop, calls=%fused_computation.11 | loop fusion | flops 28385280 | bytes 4300800 | tf_op jit(solution)/shard_map/convert_element_type | solution.py:15
  175.1 0.6 copy.19
  175.8 0.5 reshape.25
  176.3 0.2 copy.20
  176.5 2.6 %reshape.26 = bf16[256,16,105]{2,1,0:T(8,128)(2,1)S(1)} reshape(bf16[16,16,5,336]{3,2,1,0:T(8,128)(2,1)S(1)} %copy.20) | data formatting | bytes 1720320 | tf_op jit(solution)/shard_map/reshape | solution.py:49
  179.1 41.8 %all_to_all.11 = bf16[256,16,105]{2,1,0:T(8,128)(2,1)S(1)} all-to-all(bf16[256,16,105]{2,1,0:T(8,128)(2,1)S(1)} %reshape.26), channel_id=1, replica_groups=mesh['expert'=16,'fsdp'=16] {'expert','fsdp'}, dimensions={0} | all-to-all | bytes 1720320 | tf_op jit(solution)/shard_map/all_to_all | solution.py:50
  220.8 2.6 %reshape.27 = bf16[16,16,5,336]{3,2,1,0:T(8,128)(2,1)S(1)} reshape(bf16[256,16,105]{2,1,0:T(8,128)(2,1)S(1)} %all_to_all.11) | data formatting | bytes 1720320 | tf_op jit(solution)/shard_map/reshape | solution.py:51
  223.4 0.0 copy-start.1
  223.4 0.1 copy.21
  223.6 1.2 reshape.29
  224.7 0.0 copy-done.1
  224.8 0.4 fusion.4
  225.1 1.2 copy.22
Async XLA Ops:
  6.5 2.2 copy-start
  6.5 149.3 %all-gather.2.cloned.1.call-start = ((), (), s32[]{:S(2)}) async-start(), calls=%async_computation.2 | async-start | bytes 16711680 | tf_op jit(solution)/shard_map/all_gather | solution.py:44
  223.4 1.3 copy-start.1
Sparse Core Ops, SparseCore 0:
  48.1 107.6 all-gather.1

commit v5 on v4

--- a/solution.py
+++ b/solution.py
@@ -46,9 +46,12 @@
         up_rows,
     )
     shaped = local_hidden.reshape(fsdp_size, experts, cap_slots, columns)
-    by_owner = jnp.transpose(shaped, (1, 0, 2, 3)).reshape(experts * fsdp_size, 16, -1)
+    wide = -(-columns // 128) * 128
+    by_owner = jnp.transpose(shaped, (1, 0, 2, 3))
+    by_owner = jnp.pad(by_owner, ((0, 0), (0, 0), (0, 0), (0, wide - columns)))
+    by_owner = by_owner.reshape(experts * fsdp_size, cap_slots * wide // 128, 128)
     returned = lax.all_to_all(by_owner, ("expert", "fsdp"), 0, 0, tiled=True)
-    returned = returned.reshape(experts, fsdp_size, cap_slots, columns)
+    returned = returned.reshape(experts, fsdp_size, cap_slots, wide)[..., :columns]
     returned = jnp.transpose(returned, (0, 2, 1, 3)).reshape(experts * cap_slots, -1)
     collected = lax.dot_general(
         placing, returned, (((2,), (0,)), ((), ())), preferred_element_type=jnp.float32

time: 233 us -> 232 us (level)
  no operation moved by 1% of the time
where the time goes in v5:
time: 232 us
  waiting for transfers between devices  108 us (47%)
  blocking collectives  78.8 us (34%)
  matrix products  16.4 us (7%)
  between operations  13.5 us (6%)
  local copies, waits for them, and re-layouts  10.1 us (4%)
  other arithmetic  4.92 us (2%)
    all_gather x1, waiting for transfers between devices, local(): lax.all_gather(arrived.reshape(-1, model_width), 'fsdp', axis=0, tiled=True)  108 us
    all_to_all x1, blocking collectives, local(): returned = lax.all_to_all(by_owner, ('expert', 'fsdp'), 0, 0, tiled=True)  41.9 us
    all_to_all x1, blocking collectives, local(): lax.all_to_all(dense, 'expert', split_axis=0, concat_axis=0, tiled=True)  36.9 us
    dot_general x1, matrix products, hidden_block(): lax.dot_general(row_block, both, (((1,), (1,)), ((), ())), preferred_elem...  15.5 us
  transfers between devices with their start and end apart: 1, of which 1 were waited for; matrix products, arithmetic and copies ran while one was open for 0% of the time, Pallas kernels for 0%

profile of v5, /device:TPU:1, one launch (start us, length us, event | category | flops | bytes accessed | tf_op | source)
XLA Modules:
  0.0 231.5 jit_solution(13042834220327679037)
XLA Ops:
  6.5 0.0 copy-start
  6.5 0.0 all-gather.2.cloned.1.call-start
  6.5 0.8 copy.17
  7.3 0.1 eq.28
  7.4 0.1 fusion.17
  7.5 0.1 reduce_window_sum.11
  7.6 0.2 select_reduce_fusion
  7.8 0.1 reduce_sum.24
  7.9 0.1 copy.18
  8.0 0.7 multiply_add_fusion
  8.7 0.1 fusion.18
  8.7 0.0 copy-done
  8.8 0.4 convolution_convert_fusion
  9.2 0.4 reshape_reshape.3
  9.7 36.9 %all_to_all.10 = bf16[16,240,128]{2,1,0:T(8,128)(2,1)S(1)} all-to-all(bf16[16,240,128]{2,1,0:T(8,128)(2,1)S(1)} %reshape_reshape.3), channel_id=1, replica_groups=mesh['expert'=16,'fsdp'=16] {'expert'}, dimensions={0} | all-to-all | bytes 1966080 | tf_op jit(solution)/shard_map/all_to_all | solution.py:42
  46.6 1.4 reshape.24
  48.0 0.0 all-gather.2.cloned.1.call-update
  48.0 107.8 %all-gather.2.cloned.1.call-done = bf16[1280,6144]{1,0:T(8,128)(2,1)} async-done(((bf16[80,6144]{1,0:T(8,128)(2,1)}), bf16[1280,6144]{1,0:T(8,128)(2,1)}) %all-gather.2.cloned.1.call-update) | async-done | bytes 15728656 | tf_op jit(solution)/shard_map/all_gather | solution.py:44
  155.8 15.5 %fusion = f32[1280,672]{0,1:T(8,128)S(1)} fusion(bf16[1280,6144]{1,0:T(8,128)(2,1)} %all-gather.2.cloned.1.call-done, bf16[336,6144]{1,0:T(8,128)(2,1)} %bitcast.12, bf16[336,6144]{1,0:T(8,128)(2,1)} %bitcast.13), kind=kOutput, calls=%fused_computation | convolution fusion | flops 10586161152 | bytes 27426816 | tf_op jit(solution)/shard_map/dot_general | solution.py:10
  171.3 3.8 %fusion.8 = bf16[1280,336]{0,1:T(8,128)(2,1)S(1)} fusion(f32[1280,672]{0,1:T(8,128)S(1)} %fusion), kind=kLoop, calls=%fused_computation.11 | loop fusion | flops 28385280 | bytes 4300800 | tf_op jit(solution)/shard_map/convert_element_type | solution.py:15
  175.1 0.6 copy.19
  175.8 0.5 reshape.25
  176.3 0.2 copy.23
  176.5 0.4 pad.4.clone
  176.9 0.6 reshape.26
  177.4 41.9 %all_to_all.11 = bf16[256,15,128]{2,1,0:T(8,128)(2,1)} all-to-all(bf16[256,15,128]{2,1,0:T(8,128)(2,1)S(1)} %reshape.26), channel_id=1, replica_groups=mesh['expert'=16,'fsdp'=16] {'expert','fsdp'}, dimensions={0} | all-to-all | bytes 1966080 | tf_op jit(solution)/shard_map/all_to_all | solution.py:53
  219.3 2.3 reshape.27
  221.6 0.2 slice_bitcast_fusion
  221.8 0.0 copy-start.1
  221.8 0.1 copy.21
  221.9 1.2 reshape.29
  223.1 0.0 copy-done.1
  223.1 0.4 fusion.4
  223.5 1.2 copy.22
Async XLA Ops:
  6.5 2.2 copy-start
  6.5 149.3 %all-gather.2.cloned.1.call-start = ((), (), s32[]{:S(2)}) async-start(), calls=%async_computation.2 | async-start | bytes 16711680 | tf_op jit(solution)/shard_map/all_gather | solution.py:44
  221.8 1.3 copy-start.1
Sparse Core Ops, SparseCore 0:
  48.1 107.6 all-gather.1

commit v6 on v5

--- a/solution.py
+++ b/solution.py
@@ -2,17 +2,40 @@
 import jax.numpy as jnp
 from jax import lax
 from jax.sharding import PartitionSpec as P
+from jax.experimental import pallas as pl
+from jax.experimental.pallas import tpu as pltpu
+
+
+def _hidden_kernel(rows_ref, gate_ref, up_ref, out_ref):
+    rows = rows_ref[...]
+    dims = (((1,), (1,)), ((), ()))
+    gate_act = lax.dot_general(rows, gate_ref[...], dims, preferred_element_type=jnp.float32)
+    up_act = lax.dot_general(rows, up_ref[...], dims, preferred_element_type=jnp.float32)
+    gelu = gate_act * (1.0 + lax.erf(gate_act * (2.0 ** -0.5))) * 0.5
+    out_ref[...] = (gelu * up_act).astype(out_ref.dtype)
 
 
 def hidden_block(row_block, gate_rows, up_rows):
+    count, width = row_block.shape
     columns = gate_rows.shape[0]
-    both = jnp.concatenate([gate_rows, up_rows], axis=0)
-    acts = lax.dot_general(
-        row_block, both, (((1,), (1,)), ((), ())), preferred_element_type=jnp.float32
-    )
-    gate_act = acts[:, :columns]
-    up_act = acts[:, columns:]
-    return (jax.nn.gelu(gate_act, approximate=False) * up_act).astype(jnp.bfloat16)
+    tile = 128
+    return pl.pallas_call(
+        _hidden_kernel,
+        grid=(count // tile,),
+        in_specs=[
+            pl.BlockSpec((tile, width), lambda i: (i, 0)),
+            pl.BlockSpec(memory_space=pltpu.VMEM),
+            pl.BlockSpec(memory_space=pltpu.VMEM),
+        ],
+        out_specs=pl.BlockSpec((tile, columns), lambda i: (i, 0)),
+        out_shape=jax.ShapeDtypeStruct((count, columns), jnp.bfloat16),
+        compiler_params=pltpu.CompilerParams(vmem_limit_bytes=48 * 1024 * 1024),
+        cost_estimate=pl.CostEstimate(
+            flops=4 * count * width * columns,
+            transcendentals=count * columns,
+            bytes_accessed=2 * (count * width + 2 * columns * width + count * columns),
+        ),
+    )(row_block, gate_rows, up_rows)
 
 
 def local(tokens, expert_ids, router_weight, w_gate, w_up):

time: 232 us -> 244 us (1.052)
  Pallas kernels: 0 us -> 30.3 us
  matrix products: 16.4 us -> 0.81 us
  other arithmetic: 4.92 us -> 1.13 us
    pallas_call x0 -> x1, Pallas kernels: none -> 30.3 us  [hidden_block(): pl.pallas_call(_hidden_kernel, grid=(count // tile,), in_specs=[pl.BlockS...]
    dot_general x1 -> x0, matrix products: 15.5 us -> none  [hidden_block(): lax.dot_general(row_block, both, (((1,), (1,)), ((), ())), preferred_elem...]
    convert_element_type x1 -> x0, other arithmetic: 3.79 us -> none  [hidden_block(): (jax.nn.gelu(gate_act, approximate=False) * up_act).astype(jnp.bfloat16)]
where the time goes in v6:
time: 244 us
  waiting for transfers between devices  108 us (44%)
  blocking collectives  78.8 us (32%)
  Pallas kernels  30.3 us (12%)
  between operations  13.5 us (6%)
  local copies, waits for them, and re-layouts  11.7 us (5%)
    all_gather x1, waiting for transfers between devices, local(): lax.all_gather(arrived.reshape(-1, model_width), 'fsdp', axis=0, tiled=True)  108 us
    all_to_all x1, blocking collectives, local(): returned = lax.all_to_all(by_owner, ('expert', 'fsdp'), 0, 0, tiled=True)  41.9 us
    all_to_all x1, blocking collectives, local(): lax.all_to_all(dense, 'expert', split_axis=0, concat_axis=0, tiled=True)  36.9 us
    pallas_call x1, Pallas kernels, hidden_block(): pl.pallas_call(_hidden_kernel, grid=(count // tile,), in_specs=[pl.BlockS...  30.3 us
  transfers between devices with their start and end apart: 1, of which 1 were waited for; matrix products, arithmetic and copies ran while one was open for 0% of the time, Pallas kernels for 0%

profile of v6, /device:TPU:1, one launch (start us, length us, event | category | flops | bytes accessed | tf_op | source)
XLA Modules:
  0.0 244.0 jit_solution(15067749574609457306)
XLA Ops:
  6.5 0.0 copy-start
  6.5 0.0 all-gather.2.cloned.1.call-start
  6.5 0.8 copy.16
  7.3 0.1 eq.28
  7.4 0.1 fusion.2
  7.5 0.1 reduce_window_sum.11
  7.6 0.2 select_reduce_fusion
  7.8 0.1 reduce_sum.24
  7.9 0.1 copy.17
  8.0 0.7 multiply_add_fusion
  8.7 0.1 fusion.3
  8.7 0.0 copy-done
  8.8 0.4 convolution_convert_fusion
  9.2 0.4 reshape_reshape.3
  9.6 36.9 %all_to_all.10 = bf16[16,240,128]{2,1,0:T(8,128)(2,1)S(1)} all-to-all(bf16[16,240,128]{2,1,0:T(8,128)(2,1)S(1)} %reshape_reshape.3), channel_id=1, replica_groups=mesh['expert'=16,'fsdp'=16] {'expert'}, dimensions={0} | all-to-all | bytes 1966080 | tf_op jit(solution)/shard_map/all_to_all | solution.py:65
  46.6 1.4 reshape.24
  48.0 0.0 all-gather.2.cloned.1.call-update
  48.0 107.8 %all-gather.2.cloned.1.call-done.rows_ref = bf16[1280,6144]{1,0:T(8,128)(2,1)} async-done(((bf16[80,6144]{1,0:T(8,128)(2,1)}), bf16[1280,6144]{1,0:T(8,128)(2,1)}) %all-gather.2.cloned.1.call-update) | async-done | bytes 15728656 | tf_op jit(solution)/shard_map/all_gather | solution.py:67
  155.8 0.0 copy-start.1
  155.8 2.2 copy-done.1
  158.0 30.3 %shard_map.55 = bf16[1280,336]{1,0:T(8,128)(2,1)S(1)} custom-call(bf16[1280,6144]{1,0:T(8,128)(2,1)} %all-gather.2.cloned.1.call-done.rows_ref, bf16[336,6144]{1,0:T(8,128)(2,1)S(1)} %bitcast.10, bf16[336,6144]{1,0:T(8,128)(2,1)} %bitcast.12), custom_call_target="tpu_custom_call" | custom-call | flops 10569646080 | bytes 24846336 | tf_op jit(solution)/shard_map/pallas_call | solution.py:22
  188.3 0.5 reshape.25
  188.8 0.2 copy.21
  189.0 0.4 pad.4.clone
  189.4 0.6 reshape.26
  189.9 41.9 %all_to_all.11 = bf16[256,15,128]{2,1,0:T(8,128)(2,1)} all-to-all(bf16[256,15,128]{2,1,0:T(8,128)(2,1)S(1)} %reshape.26), channel_id=1, replica_groups=mesh['expert'=16,'fsdp'=16] {'expert','fsdp'}, dimensions={0} | all-to-all | bytes 1966080 | tf_op jit(solution)/shard_map/all_to_all | solution.py:76
  231.8 2.3 reshape.27
  234.1 0.2 slice_bitcast_fusion
  234.3 0.0 copy-start.2
  234.3 0.1 copy.19
  234.4 1.2 reshape.29
  235.6 0.0 copy-done.2
  235.6 0.4 fusion
  236.0 1.2 copy.20
Async XLA Ops:
  6.5 2.2 copy-start
  6.5 149.3 %all-gather.2.cloned.1.call-start = ((), (), s32[]{:S(2)}) async-start(), calls=%async_computation.2 | async-start | bytes 16711680 | tf_op jit(solution)/shard_map/all_gather | solution.py:67
  155.8 2.2 copy-start.1
  234.3 1.3 copy-start.2
Sparse Core Ops, SparseCore 0:
  48.1 107.6 all-gather.1

commit v7 on v6

--- a/solution.py
+++ b/solution.py
@@ -8,9 +8,8 @@
 
 def _hidden_kernel(rows_ref, gate_ref, up_ref, out_ref):
     rows = rows_ref[...]
-    dims = (((1,), (1,)), ((), ()))
-    gate_act = lax.dot_general(rows, gate_ref[...], dims, preferred_element_type=jnp.float32)
-    up_act = lax.dot_general(rows, up_ref[...], dims, preferred_element_type=jnp.float32)
+    gate_act = jnp.dot(rows, gate_ref[...], preferred_element_type=jnp.float32)
+    up_act = jnp.dot(rows, up_ref[...], preferred_element_type=jnp.float32)
     gelu = gate_act * (1.0 + lax.erf(gate_act * (2.0 ** -0.5))) * 0.5
     out_ref[...] = (gelu * up_act).astype(out_ref.dtype)
 
@@ -18,7 +17,7 @@
 def hidden_block(row_block, gate_rows, up_rows):
     count, width = row_block.shape
     columns = gate_rows.shape[0]
-    tile = 128
+    tile = 256
     return pl.pallas_call(
         _hidden_kernel,
         grid=(count // tile,),
@@ -35,7 +34,7 @@
             transcendentals=count * columns,
             bytes_accessed=2 * (count * width + 2 * columns * width + count * columns),
         ),
-    )(row_block, gate_rows, up_rows)
+    )(row_block, gate_rows.T, up_rows.T)
 
 
 def local(tokens, expert_ids, router_weight, w_gate, w_up):

time: 244 us -> 235 us (0.963)
  waiting for transfers between devices: 108 us -> 94.8 us
  local copies, waits for them, and re-layouts: 11.7 us -> 24.9 us
  Pallas kernels: 30.3 us -> 20.7 us
    unnamed x8 -> x10, local copies, waits for them, and re-layouts: 3.21 us -> 16.4 us
    all_gather x1, waiting for transfers between devices: 108 us -> 94.8 us  [local(): lax.all_gather(arrived.reshape(-1, model_width), 'fsdp', axis=0, tiled=True)]
    pallas_call x1, Pallas kernels: 30.3 us -> 20.7 us  [hidden_block(): pl.pallas_call(_hidden_kernel, grid=(count // tile,), in_specs=[pl.BlockS...]
  transfers between devices with their start and end apart: 1 -> 1, of which waited for: 1 -> 1; matrix products, arithmetic and copies ran while one was open for 0% -> 6% of each run, Pallas kernels for 0% -> 0%
where the time goes in v7:
time: 235 us
  waiting for transfers between devices  94.8 us (40%)
  blocking collectives  78.8 us (34%)
  local copies, waits for them, and re-layouts  24.9 us (11%)
  Pallas kernels  20.7 us (9%)
  between operations  13.5 us (6%)
    all_gather x1, waiting for transfers between devices, local(): lax.all_gather(arrived.reshape(-1, model_width), 'fsdp', axis=0, tiled=True)  94.8 us
    all_to_all x1, blocking collectives, local(): returned = lax.all_to_all(by_owner, ('expert', 'fsdp'), 0, 0, tiled=True)  41.9 us
    all_to_all x1, blocking collectives, local(): lax.all_to_all(dense, 'expert', split_axis=0, concat_axis=0, tiled=True)  36.9 us
    pallas_call x1, Pallas kernels, hidden_block(): pl.pallas_call(_hidden_kernel, grid=(count // tile,), in_specs=[pl.BlockS...  20.7 us
    unnamed x10, local copies, waits for them, and re-layouts  16.4 us
  transfers between devices with their start and end apart: 1, of which 1 were waited for; matrix products, arithmetic and copies ran while one was open for 6% of the time, Pallas kernels for 0%

profile of v7, /device:TPU:1, one launch (start us, length us, event | category | flops | bytes accessed | tf_op | source)
XLA Modules:
  0.0 234.7 jit_solution(16987854691430549251)
XLA Ops:
  6.5 0.0 copy-start
  6.5 0.0 all-gather.2.cloned.1.call-start
  6.5 0.8 copy.20
  7.3 0.1 eq.28
  7.4 0.1 fusion.2
  7.5 0.1 reduce_window_sum.11
  7.6 0.2 select_reduce_fusion
  7.8 0.1 reduce_sum.24
  7.9 0.1 copy.21
  8.0 0.7 multiply_add_fusion
  8.7 0.1 fusion.3
  8.7 0.0 copy-done
  8.8 0.4 convolution_convert_fusion
  9.2 0.4 reshape_reshape.3
  9.6 36.9 %all_to_all.10 = bf16[16,240,128]{2,1,0:T(8,128)(2,1)S(1)} all-to-all(bf16[16,240,128]{2,1,0:T(8,128)(2,1)S(1)} %reshape_reshape.3), channel_id=1, replica_groups=mesh['expert'=16,'fsdp'=16] {'expert'}, dimensions={0} | all-to-all | bytes 1966080 | tf_op jit(solution)/shard_map/all_to_all | solution.py:64
  46.6 1.4 reshape.24
  48.0 0.0 all-gather.2.cloned.1.call-update
  48.0 6.5 %copy.22 = bf16[1,336,6144]{1,2,0:T(8,128)(2,1)} copy(bf16[1,336,6144]{2,1,0:T(8,128)(2,1)} %param.8) | data formatting | bytes 8257536 | tf_op args[3]
  54.5 6.5 %copy.23 = bf16[1,336,6144]{1,2,0:T(8,128)(2,1)} copy(bf16[1,336,6144]{2,1,0:T(8,128)(2,1)} %param.9) | data formatting | bytes 8257536 | tf_op args[4]
  61.0 94.8 %all-gather.2.cloned.1.call-done.rows_ref = bf16[1280,6144]{1,0:T(8,128)(2,1)} async-done(((bf16[80,6144]{1,0:T(8,128)(2,1)}), bf16[1280,6144]{1,0:T(8,128)(2,1)}) %all-gather.2.cloned.1.call-update) | async-done | bytes 15728656 | tf_op jit(solution)/shard_map/all_gather | solution.py:66
  155.9 0.0 copy-start.1
  155.9 2.3 copy-done.1
  158.2 20.7 %shard_map.55 = bf16[1280,336]{1,0:T(8,128)(2,1)S(1)} custom-call(bf16[1280,6144]{1,0:T(8,128)(2,1)} %all-gather.2.cloned.1.call-done.rows_ref, bf16[6144,336]{1,0:T(8,128)(2,1)S(1)} %bitcast.14, bf16[6144,336]{1,0:T(8,128)(2,1)} %bitcast.16), custom_call_target="tpu_custom_call" | custom-call | flops 10569646080 | bytes 24846336 | tf_op jit(solution)/shard_map/pallas_call | solution.py:21
  178.9 0.5 reshape.25
  179.4 0.2 copy.27
  179.6 0.4 pad.4.clone
  180.0 0.6 reshape.26
  180.6 41.9 %all_to_all.11 = bf16[256,15,128]{2,1,0:T(8,128)(2,1)} all-to-all(bf16[256,15,128]{2,1,0:T(8,128)(2,1)S(1)} %reshape.26), channel_id=1, replica_groups=mesh['expert'=16,'fsdp'=16] {'expert','fsdp'}, dimensions={0} | all-to-all | bytes 1966080 | tf_op jit(solution)/shard_map/all_to_all | solution.py:75
  222.4 2.3 reshape.27
  224.7 0.2 slice_bitcast_fusion
  224.9 0.0 copy-start.2
  224.9 0.1 copy.25
  225.0 1.2 reshape.29
  226.2 0.0 copy-done.2
  226.2 0.4 fusion
  226.6 1.2 copy.26
Async XLA Ops:
  6.5 2.2 copy-start
  6.5 149.3 %all-gather.2.cloned.1.call-start = ((), (), s32[]{:S(2)}) async-start(), calls=%async_computation.2 | async-start | bytes 16711680 | tf_op jit(solution)/shard_map/all_gather | solution.py:66
  155.9 2.3 copy-start.1
  224.9 1.3 copy-start.2
Sparse Core Ops, SparseCore 0:
  48.2 107.6 all-gather.1

commit v8 on v5

--- a/solution.py
+++ b/solution.py
@@ -53,10 +53,8 @@
     returned = lax.all_to_all(by_owner, ("expert", "fsdp"), 0, 0, tiled=True)
     returned = returned.reshape(experts, fsdp_size, cap_slots, wide)[..., :columns]
     returned = jnp.transpose(returned, (0, 2, 1, 3)).reshape(experts * cap_slots, -1)
-    collected = lax.dot_general(
-        placing, returned, (((2,), (0,)), ((), ())), preferred_element_type=jnp.float32
-    )
-    return (router_weight[:, :, None] * collected).astype(jnp.bfloat16)
+    collected = jnp.take(returned, slot_of.reshape(tok_rows, top_count), axis=0, mode="clip")
+    return (router_weight[:, :, None] * collected.astype(jnp.float32)).astype(jnp.bfloat16)
 
 
 def solution(mesh):

time: 232 us -> 231 us (level)
  blocking collectives: 78.8 us -> 36.9 us
  waiting for transfers between devices: 108 us -> 138 us
  starting transfers between devices: 0.01 us -> 11.6 us
    all_to_all x1 -> x0, blocking collectives: 41.9 us -> none  [local(): returned = lax.all_to_all(by_owner, ('expert', 'fsdp'), 0, 0, tiled=True)]
    all_to_all x0 -> x1, waiting for transfers between devices: none -> 30.1 us  [local(): returned = lax.all_to_all(by_owner, ('expert', 'fsdp'), 0, 0, tiled=True)]
    all_to_all x0 -> x1, starting transfers between devices: none -> 11.6 us  [local(): returned = lax.all_to_all(by_owner, ('expert', 'fsdp'), 0, 0, tiled=True)]
  transfers between devices with their start and end apart: 1 -> 2, of which waited for: 1 -> 2; matrix products, arithmetic and copies ran while one was open for 0% -> 0% of each run, Pallas kernels for 0% -> 0%
where the time goes in v8:
time: 231 us
  waiting for transfers between devices  138 us (60%)
  blocking collectives  36.9 us (16%)
  matrix products  15.9 us (7%)
  between operations  13.6 us (6%)
  starting transfers between devices  11.6 us (5%)
  local copies, waits for them, and re-layouts  9.5 us (4%)
  other arithmetic  5.4 us (2%)
    all_gather x1, waiting for transfers between devices, local(): lax.all_gather(arrived.reshape(-1, model_width), 'fsdp', axis=0, tiled=True)  108 us
    all_to_all x1, blocking collectives, local(): lax.all_to_all(dense, 'expert', split_axis=0, concat_axis=0, tiled=True)  36.9 us
    all_to_all x1, waiting for transfers between devices, local(): returned = lax.all_to_all(by_owner, ('expert', 'fsdp'), 0, 0, tiled=True)  30.1 us
    dot_general x1, matrix products, hidden_block(): lax.dot_general(row_block, both, (((1,), (1,)), ((), ())), preferred_elem...  15.5 us
    all_to_all x1, starting transfers between devices, local(): returned = lax.all_to_all(by_owner, ('expert', 'fsdp'), 0, 0, tiled=True)  11.6 us
  transfers between devices with their start and end apart: 2, of which 2 were waited for; matrix products, arithmetic and copies ran while one was open for 0% of the time, Pallas kernels for 0%

profile of v8, /device:TPU:1, one launch (start us, length us, event | category | flops | bytes accessed | tf_op | source)
XLA Modules:
  0.0 231.0 jit_solution(1867955087364790801)
XLA Ops:
  6.5 0.0 copy-start
  6.5 0.0 all-gather.2.cloned.1.call-start
  6.5 0.8 copy.16
  7.3 0.1 eq.28
  7.4 0.1 fusion.15
  7.5 0.1 reduce_window_sum.11
  7.6 0.2 select_reduce_fusion
  7.8 0.1 reduce_sum.24
  7.9 0.1 copy.18
  8.0 0.1 fusion.17
  8.1 0.0 copy-done
  8.1 0.4 convolution_convert_fusion
  8.5 0.4 reshape_reshape.3
  9.0 36.9 %all_to_all.10 = bf16[16,240,128]{2,1,0:T(8,128)(2,1)S(1)} all-to-all(bf16[16,240,128]{2,1,0:T(8,128)(2,1)S(1)} %reshape_reshape.3), channel_id=1, replica_groups=mesh['expert'=16,'fsdp'=16] {'expert'}, dimensions={0} | all-to-all | bytes 1966080 | tf_op jit(solution)/shard_map/all_to_all | solution.py:42
  45.9 1.4 reshape.28
  47.3 0.0 all-gather.2.cloned.1.call-update
  47.3 107.8 %all-gather.2.cloned.1.call-done = bf16[1280,6144]{1,0:T(8,128)(2,1)} async-done(((bf16[80,6144]{1,0:T(8,128)(2,1)}), bf16[1280,6144]{1,0:T(8,128)(2,1)}) %all-gather.2.cloned.1.call-update) | async-done | bytes 15728656 | tf_op jit(solution)/shard_map/all_gather | solution.py:44
  155.1 15.5 %fusion = f32[1280,672]{0,1:T(8,128)S(1)} fusion(bf16[1280,6144]{1,0:T(8,128)(2,1)} %all-gather.2.cloned.1.call-done, bf16[336,6144]{1,0:T(8,128)(2,1)} %bitcast.11, bf16[336,6144]{1,0:T(8,128)(2,1)} %bitcast.12), kind=kOutput, calls=%fused_computation.1 | convolution fusion | flops 10586161152 | bytes 27426816 | tf_op jit(solution)/shard_map/dot_general | solution.py:10
  170.7 3.8 %fusion.7 = bf16[1280,336]{0,1:T(8,128)(2,1)S(1)} fusion(f32[1280,672]{0,1:T(8,128)S(1)} %fusion), kind=kLoop, calls=%fused_computation.10 | loop fusion | flops 28385280 | bytes 4300800 | tf_op jit(solution)/shard_map/convert_element_type | solution.py:15
  174.5 0.6 copy.19
  175.1 0.5 reshape.29
  175.6 0.2 copy.22
  175.8 0.4 pad.4.clone
  176.2 0.0 copy-start.1
  176.3 1.4 reshape.30
  177.6 11.6 %all-to-all-start.1 = ((bf16[256,15,128]{2,1,0:T(8,128)(2,1)}), bf16[256,15,128]{2,1,0:T(8,128)(2,1)S(1)}, u32[]{:S(2)}, u32[]{:S(2)}) async-start(bf16[256,15,128]{2,1,0:T(8,128)(2,1)} %reshape.30), calls=%async_computation.1 | async-start | bytes 2097152 | tf_op jit(solution)/shard_map/all_to_all | solution.py:53
  189.3 0.1 reshape.35
  189.4 0.0 copy-done.1
  189.4 0.1 copy.15
  189.5 30.1 %all-to-all-done.1 = bf16[256,15,128]{2,1,0:T(8,128)(2,1)S(1)} async-done(((bf16[256,15,128]{2,1,0:T(8,128)(2,1)}), bf16[256,15,128]{2,1,0:T(8,128)(2,1)S(1)}, u32[]{:S(2)}, u32[]{:S(2)}) %all-to-all-start.1) | async-done | bytes 983072 | tf_op jit(solution)/shard_map/all_to_all | solution.py:53
  219.6 0.5 reshape.31
  220.1 0.2 slice_bitcast_fusion
  220.3 0.1 copy.21
  220.4 1.2 reshape.32
  221.6 1.0 gather_fusion
  222.6 0.3 reshape.43
  223.0 1.2 multiply_convert_fusion
  (2 shorter events, 0.0 us)
Async XLA Ops:
  6.5 1.5 copy-start
  6.5 148.6 %all-gather.2.cloned.1.call-start = ((), (), s32[]{:S(2)}) async-start(), calls=%async_computation.2 | async-start | bytes 16711680 | tf_op jit(solution)/shard_map/all_gather | solution.py:44
  176.2 13.1 %copy-start.1 = (f32[16,4]{0,1:T(4,128)S(1)}, f32[16,4]{0,1:T(4,128)}, u32[]{:S(2)}) copy-start(f32[16,4]{0,1:T(4,128)} %param.7) | copy-start | bytes 772
  177.6 42.0 %all-to-all-start.1 = ((bf16[256,15,128]{2,1,0:T(8,128)(2,1)}), bf16[256,15,128]{2,1,0:T(8,128)(2,1)S(1)}, u32[]{:S(2)}, u32[]{:S(2)}) async-start(bf16[256,15,128]{2,1,0:T(8,128)(2,1)} %reshape.30), calls=%async_computation.1 | async-start | bytes 2097152 | tf_op jit(solution)/shard_map/all_to_all | solution.py:53
Sparse Core Ops, SparseCore 0:
  47.4 107.6 all-gather.1

commit v9 on v8

--- a/solution.py
+++ b/solution.py
@@ -22,10 +22,9 @@
     fsdp_size = lax.axis_size("fsdp")
     cap_slots = 5 * tok_rows * top_count // (4 * experts)
     flat_ids = expert_ids.reshape(-1)
-    choosing = (flat_ids[:, None] == jnp.arange(experts, dtype=jnp.int32)[None, :]).astype(
-        jnp.int32
-    )
-    slot_rank = jnp.sum((jnp.cumsum(choosing, axis=0) - 1) * choosing, axis=1)
+    order = jnp.arange(flat_ids.shape[0], dtype=jnp.int32)
+    earlier = (order[None, :] < order[:, None]) & (flat_ids[None, :] == flat_ids[:, None])
+    slot_rank = jnp.sum(earlier.astype(jnp.int32), axis=1)
     slot_of = flat_ids * cap_slots + slot_rank
     slots = jnp.arange(experts * cap_slots, dtype=jnp.int32)
     placing = (slot_of.reshape(tok_rows, top_count)[:, :, None] == slots).astype(jnp.bfloat16)

time: 231 us -> 231 us (level)
  no operation moved by 1% of the time
where the time goes in v9:
time: 231 us
  waiting for transfers between devices  138 us (60%)
  blocking collectives  36.9 us (16%)
  matrix products  16 us (7%)
  between operations  13.6 us (6%)
  starting transfers between devices  11.6 us (5%)
  local copies, waits for them, and re-layouts  9.49 us (4%)
  other arithmetic  5.23 us (2%)
    all_gather x1, waiting for transfers between devices, local(): lax.all_gather(arrived.reshape(-1, model_width), 'fsdp', axis=0, tiled=True)  108 us
    all_to_all x1, blocking collectives, local(): lax.all_to_all(dense, 'expert', split_axis=0, concat_axis=0, tiled=True)  36.9 us
    all_to_all x1, waiting for transfers between devices, local(): returned = lax.all_to_all(by_owner, ('expert', 'fsdp'), 0, 0, tiled=True)  30.1 us
    dot_general x1, matrix products, hidden_block(): lax.dot_general(row_block, both, (((1,), (1,)), ((), ())), preferred_elem...  15.5 us
    all_to_all x1, starting transfers between devices, local(): returned = lax.all_to_all(by_owner, ('expert', 'fsdp'), 0, 0, tiled=True)  11.6 us
  transfers between devices with their start and end apart: 2, of which 2 were waited for; matrix products, arithmetic and copies ran while one was open for 0% of the time, Pallas kernels for 0%

profile of v9, /device:TPU:1, one launch (start us, length us, event | category | flops | bytes accessed | tf_op | source)
XLA Modules:
  0.0 230.8 jit_solution(140213789234228741)
XLA Ops:
  6.5 0.0 copy-start
  6.5 0.0 all-gather.2.cloned.1.call-start
  6.5 0.8 copy.16
  7.3 0.1 eq.28
  7.4 0.2 convert_reduce_fusion
  7.6 0.1 reduce_sum.24
  7.7 0.1 copy.18
  7.8 0.1 fusion.17
  7.9 0.0 copy-done
  7.9 0.4 convolution_convert_fusion
  8.3 0.4 reshape_reshape.3
  8.8 36.9 %all_to_all.10 = bf16[16,240,128]{2,1,0:T(8,128)(2,1)S(1)} all-to-all(bf16[16,240,128]{2,1,0:T(8,128)(2,1)S(1)} %reshape_reshape.3), channel_id=1, replica_groups=mesh['expert'=16,'fsdp'=16] {'expert'}, dimensions={0} | all-to-all | bytes 1966080 | tf_op jit(solution)/shard_map/all_to_all | solution.py:41
  45.7 1.4 reshape.29
  47.1 0.0 all-gather.2.cloned.1.call-update
  47.1 107.8 %all-gather.2.cloned.1.call-done = bf16[1280,6144]{1,0:T(8,128)(2,1)} async-done(((bf16[80,6144]{1,0:T(8,128)(2,1)}), bf16[1280,6144]{1,0:T(8,128)(2,1)}) %all-gather.2.cloned.1.call-update) | async-done | bytes 15728656 | tf_op jit(solution)/shard_map/all_gather | solution.py:43
  155.0 15.5 %fusion = f32[1280,672]{0,1:T(8,128)S(1)} fusion(bf16[1280,6144]{1,0:T(8,128)(2,1)} %all-gather.2.cloned.1.call-done, bf16[336,6144]{1,0:T(8,128)(2,1)} %bitcast.11, bf16[336,6144]{1,0:T(8,128)(2,1)} %bitcast.12), kind=kOutput, calls=%fused_computation.1 | convolution fusion | flops 10586161152 | bytes 27426816 | tf_op jit(solution)/shard_map/dot_general | solution.py:10
  170.5 3.8 %fusion.7 = bf16[1280,336]{0,1:T(8,128)(2,1)S(1)} fusion(f32[1280,672]{0,1:T(8,128)S(1)} %fusion), kind=kLoop, calls=%fused_computation.10 | loop fusion | flops 28385280 | bytes 4300800 | tf_op jit(solution)/shard_map/convert_element_type | solution.py:15
  174.3 0.6 copy.19
  174.9 0.5 reshape.30
  175.4 0.2 copy.22
  175.7 0.4 pad.4.clone
  176.1 0.0 copy-start.1
  176.1 1.3 reshape.31
  177.4 11.6 %all-to-all-start.1 = ((bf16[256,15,128]{2,1,0:T(8,128)(2,1)}), bf16[256,15,128]{2,1,0:T(8,128)(2,1)S(1)}, u32[]{:S(2)}, u32[]{:S(2)}) async-start(bf16[256,15,128]{2,1,0:T(8,128)(2,1)} %reshape.31), calls=%async_computation.1 | async-start | bytes 2097152 | tf_op jit(solution)/shard_map/all_to_all | solution.py:52
  189.1 0.1 reshape.36
  189.2 0.0 copy-done.1
  189.2 0.1 copy.15
  189.3 30.1 %all-to-all-done.1 = bf16[256,15,128]{2,1,0:T(8,128)(2,1)S(1)} async-done(((bf16[256,15,128]{2,1,0:T(8,128)(2,1)}), bf16[256,15,128]{2,1,0:T(8,128)(2,1)S(1)}, u32[]{:S(2)}, u32[]{:S(2)}) %all-to-all-start.1) | async-done | bytes 983072 | tf_op jit(solution)/shard_map/all_to_all | solution.py:52
  219.4 0.5 reshape.32
  219.9 0.2 slice_bitcast_fusion
  220.1 0.1 copy.21
  220.2 1.2 reshape.33
  221.5 1.0 gather_fusion
  222.5 0.3 reshape.44
  222.8 1.2 multiply_convert_fusion
  (2 shorter events, 0.0 us)
Async XLA Ops:
  6.5 1.4 copy-start
  6.5 148.4 %all-gather.2.cloned.1.call-start = ((), (), s32[]{:S(2)}) async-start(), calls=%async_computation.2 | async-start | bytes 16711680 | tf_op jit(solution)/shard_map/all_gather | solution.py:43
  176.1 13.1 %copy-start.1 = (f32[16,4]{0,1:T(4,128)S(1)}, f32[16,4]{0,1:T(4,128)}, u32[]{:S(2)}) copy-start(f32[16,4]{0,1:T(4,128)} %param.7) | copy-start | bytes 772
  177.4 42.0 %all-to-all-start.1 = ((bf16[256,15,128]{2,1,0:T(8,128)(2,1)}), bf16[256,15,128]{2,1,0:T(8,128)(2,1)S(1)}, u32[]{:S(2)}, u32[]{:S(2)}) async-start(bf16[256,15,128]{2,1,0:T(8,128)(2,1)} %reshape.31), calls=%async_computation.1 | async-start | bytes 2097152 | tf_op jit(solution)/shard_map/all_to_all | solution.py:52
Sparse Core Ops, SparseCore 0:
  47.3 107.6 all-gather.1

commit v10 on v9

--- a/solution.py
+++ b/solution.py
@@ -27,11 +27,10 @@
     slot_rank = jnp.sum(earlier.astype(jnp.int32), axis=1)
     slot_of = flat_ids * cap_slots + slot_rank
     slots = jnp.arange(experts * cap_slots, dtype=jnp.int32)
-    placing = (slot_of.reshape(tok_rows, top_count)[:, :, None] == slots).astype(jnp.bfloat16)
-    by_token = jnp.sum(placing, axis=1)
-    outgoing = lax.dot_general(
-        by_token, tokens, (((0,), (0,)), ((), ())), preferred_element_type=jnp.float32
-    ).astype(jnp.bfloat16)
+    filled = slot_of[None, :] == slots[:, None]
+    owner = jnp.arange(flat_ids.shape[0], dtype=jnp.int32) // top_count
+    token_of = jnp.sum(jnp.where(filled, owner[None, :], 0), axis=1)
+    outgoing = jnp.take(tokens, token_of, axis=0, mode="clip")
     outgoing = outgoing.reshape(experts, cap_slots, model_width)
     gate_rows = w_gate[0]
     up_rows = w_up[0]

time: 231 us -> 231 us (level)
  no operation moved by 1% of the time
where the time goes in v10:
time: 231 us
  waiting for transfers between devices  138 us (60%)
  blocking collectives  36.9 us (16%)
  matrix products  15.5 us (7%)
  between operations  13.6 us (6%)
  starting transfers between devices  11.6 us (5%)
  local copies, waits for them, and re-layouts  10.5 us (5%)
  other arithmetic  5.25 us (2%)
    all_gather x1, waiting for transfers between devices, local(): lax.all_gather(arrived.reshape(-1, model_width), 'fsdp', axis=0, tiled=True)  108 us
    all_to_all x1, blocking collectives, local(): lax.all_to_all(dense, 'expert', split_axis=0, concat_axis=0, tiled=True)  36.9 us
    all_to_all x1, waiting for transfers between devices, local(): returned = lax.all_to_all(by_owner, ('expert', 'fsdp'), 0, 0, tiled=True)  30 us
    dot_general x1, matrix products, hidden_block(): lax.dot_general(row_block, both, (((1,), (1,)), ((), ())), preferred_elem...  15.5 us
    all_to_all x1, starting transfers between devices, local(): returned = lax.all_to_all(by_owner, ('expert', 'fsdp'), 0, 0, tiled=True)  11.6 us
  transfers between devices with their start and end apart: 2, of which 2 were waited for; matrix products, arithmetic and copies ran while one was open for 0% of the time, Pallas kernels for 0%

profile of v10, /device:TPU:1, one launch (start us, length us, event | category | flops | bytes accessed | tf_op | source)
XLA Modules:
  0.0 231.3 jit_solution(4851494013437588192)
XLA Ops:
  6.5 0.0 copy-start
  6.5 0.0 all-gather.2.cloned.1.call-start
  6.5 0.8 copy.16
  7.3 0.1 reshape.49
  7.4 0.2 convert_reduce_fusion
  7.6 0.1 select_reduce_fusion
  7.7 0.0 copy-done
  7.7 1.1 gather_fusion
  8.9 0.4 reshape_reshape.3
  9.3 36.9 %all_to_all.10 = bf16[16,240,128]{2,1,0:T(8,128)(2,1)S(1)} all-to-all(bf16[16,240,128]{2,1,0:T(8,128)(2,1)S(1)} %reshape_reshape.3), channel_id=1, replica_groups=mesh['expert'=16,'fsdp'=16] {'expert'}, dimensions={0} | all-to-all | bytes 1966080 | tf_op jit(solution)/shard_map/all_to_all | solution.py:40
  46.3 1.4 reshape.50
  47.7 0.0 all-gather.2.cloned.1.call-update
  47.7 107.8 %all-gather.2.cloned.1.call-done = bf16[1280,6144]{1,0:T(8,128)(2,1)} async-done(((bf16[80,6144]{1,0:T(8,128)(2,1)}), bf16[1280,6144]{1,0:T(8,128)(2,1)}) %all-gather.2.cloned.1.call-update) | async-done | bytes 15728656 | tf_op jit(solution)/shard_map/all_gather | solution.py:42
  155.5 15.5 %fusion = f32[1280,672]{0,1:T(8,128)S(1)} fusion(bf16[1280,6144]{1,0:T(8,128)(2,1)} %all-gather.2.cloned.1.call-done, bf16[336,6144]{1,0:T(8,128)(2,1)} %bitcast.9, bf16[336,6144]{1,0:T(8,128)(2,1)} %bitcast.10), kind=kOutput, calls=%fused_computation.2 | convolution fusion | flops 10586161152 | bytes 27426816 | tf_op jit(solution)/shard_map/dot_general | solution.py:10
  171.0 3.8 %fusion.7 = bf16[1280,336]{0,1:T(8,128)(2,1)S(1)} fusion(f32[1280,672]{0,1:T(8,128)S(1)} %fusion), kind=kLoop, calls=%fused_computation.10 | loop fusion | flops 28385280 | bytes 4300800 | tf_op jit(solution)/shard_map/convert_element_type | solution.py:15
  174.8 0.6 copy.17
  175.5 0.5 reshape.51
  176.0 0.2 copy.21
  176.2 0.4 pad.4.clone
  176.6 1.3 reshape.52
  177.9 0.0 copy-start.1
  177.9 11.6 %all-to-all-start.1 = ((bf16[256,15,128]{2,1,0:T(8,128)(2,1)}), bf16[256,15,128]{2,1,0:T(8,128)(2,1)S(1)}, u32[]{:S(2)}, u32[]{:S(2)}) async-start(bf16[256,15,128]{2,1,0:T(8,128)(2,1)} %reshape.52), calls=%async_computation.1 | async-start | bytes 2097152 | tf_op jit(solution)/shard_map/all_to_all | solution.py:51
  189.6 0.1 reduce_sum.22
  189.7 0.1 reshape.65
  189.8 0.0 copy-done.1
  189.8 0.1 copy.15
  189.9 30.0 %all-to-all-done.1 = bf16[256,15,128]{2,1,0:T(8,128)(2,1)S(1)} async-done(((bf16[256,15,128]{2,1,0:T(8,128)(2,1)}), bf16[256,15,128]{2,1,0:T(8,128)(2,1)S(1)}, u32[]{:S(2)}, u32[]{:S(2)}) %all-to-all-start.1) | async-done | bytes 983072 | tf_op jit(solution)/shard_map/all_to_all | solution.py:51
  219.9 0.5 reshape.53
  220.4 0.2 slice_bitcast_fusion
  220.6 0.1 copy.19
  220.7 1.2 reshape.54
  222.0 1.0 gather_fusion.1
  222.9 0.3 reshape.74
  223.3 1.2 multiply_convert_fusion
  (4 shorter events, 0.0 us)
Async XLA Ops:
  6.5 1.2 copy-start
  6.5 149.0 %all-gather.2.cloned.1.call-start = ((), (), s32[]{:S(2)}) async-start(), calls=%async_computation.2 | async-start | bytes 16711680 | tf_op jit(solution)/shard_map/all_gather | solution.py:42
  177.9 11.8 %copy-start.1 = (f32[16,4]{0,1:T(4,128)S(1)}, f32[16,4]{0,1:T(4,128)}, u32[]{:S(2)}) copy-start(f32[16,4]{0,1:T(4,128)} %param.7) | copy-start | bytes 772
  177.9 42.0 %all-to-all-start.1 = ((bf16[256,15,128]{2,1,0:T(8,128)(2,1)}), bf16[256,15,128]{2,1,0:T(8,128)(2,1)S(1)}, u32[]{:S(2)}, u32[]{:S(2)}) async-start(bf16[256,15,128]{2,1,0:T(8,128)(2,1)} %reshape.52), calls=%async_computation.1 | async-start | bytes 2097152 | tf_op jit(solution)/shard_map/all_to_all | solution.py:51
Sparse Core Ops, SparseCore 0:
  47.8 107.6 all-gather.1

commit v11 on v9

--- a/solution.py
+++ b/solution.py
@@ -12,7 +12,8 @@
     )
     gate_act = acts[:, :columns]
     up_act = acts[:, columns:]
-    return (jax.nn.gelu(gate_act, approximate=False) * up_act).astype(jnp.bfloat16)
+    gelu = gate_act * (1.0 + lax.erf(gate_act * (2.0 ** -0.5))) * 0.5
+    return (gelu * up_act).astype(jnp.bfloat16)
 
 
 def local(tokens, expert_ids, router_weight, w_gate, w_up):

time: 231 us -> 228 us (0.987)
  other arithmetic: 5.23 us -> 1.86 us
    convert_element_type x1, other arithmetic: 3.79 us -> 0.42 us  [hidden_block(): return (gelu * up_act).astype(jnp.bfloat16)]
where the time goes in v11:
time: 228 us; the launch traced here: 227 us
  waiting for transfers between devices  138 us (61%)
  blocking collectives  36.9 us (16%)
  matrix products  15.9 us (7%)
  between operations  13.6 us (6%)
  starting transfers between devices  11.6 us (5%)
  local copies, waits for them, and re-layouts  9.49 us (4%)
    all_gather x1, waiting for transfers between devices, local(): lax.all_gather(arrived.reshape(-1, model_width), 'fsdp', axis=0, tiled=True)  108 us
    all_to_all x1, blocking collectives, local(): lax.all_to_all(dense, 'expert', split_axis=0, concat_axis=0, tiled=True)  36.9 us
    all_to_all x1, waiting for transfers between devices, local(): returned = lax.all_to_all(by_owner, ('expert', 'fsdp'), 0, 0, tiled=True)  30.1 us
    dot_general x1, matrix products, hidden_block(): lax.dot_general(row_block, both, (((1,), (1,)), ((), ())), preferred_elem...  15.5 us
    all_to_all x1, starting transfers between devices, local(): returned = lax.all_to_all(by_owner, ('expert', 'fsdp'), 0, 0, tiled=True)  11.6 us
  transfers between devices with their start and end apart: 2, of which 2 were waited for; matrix products, arithmetic and copies ran while one was open for 0% of the time, Pallas kernels for 0%

profile of v11, /device:TPU:1, one launch (start us, length us, event | category | flops | bytes accessed | tf_op | source)
XLA Modules:
  0.0 227.4 jit_solution(17980672090251323999)
XLA Ops:
  6.5 0.0 copy-start
  6.5 0.0 all-gather.2.cloned.1.call-start
  6.5 0.8 copy.16
  7.3 0.1 eq.28
  7.4 0.2 convert_reduce_fusion
  7.6 0.1 reduce_sum.24
  7.7 0.1 copy.18
  7.8 0.1 fusion.7
  7.9 0.0 copy-done
  7.9 0.4 convolution_convert_fusion
  8.3 0.4 reshape_reshape.3
  8.8 36.9 %all_to_all.10 = bf16[16,240,128]{2,1,0:T(8,128)(2,1)S(1)} all-to-all(bf16[16,240,128]{2,1,0:T(8,128)(2,1)S(1)} %reshape_reshape.3), channel_id=1, replica_groups=mesh['expert'=16,'fsdp'=16] {'expert'}, dimensions={0} | all-to-all | bytes 1966080 | tf_op jit(solution)/shard_map/all_to_all | solution.py:42
  45.7 1.4 reshape.29
  47.1 0.0 all-gather.2.cloned.1.call-update
  47.1 107.8 %all-gather.2.cloned.1.call-done = bf16[1280,6144]{1,0:T(8,128)(2,1)} async-done(((bf16[80,6144]{1,0:T(8,128)(2,1)}), bf16[1280,6144]{1,0:T(8,128)(2,1)}) %all-gather.2.cloned.1.call-update) | async-done | bytes 15728656 | tf_op jit(solution)/shard_map/all_gather | solution.py:44
  155.0 15.5 %fusion = f32[1280,672]{0,1:T(8,128)S(1)} fusion(bf16[1280,6144]{1,0:T(8,128)(2,1)} %all-gather.2.cloned.1.call-done, bf16[336,6144]{1,0:T(8,128)(2,1)} %bitcast.11, bf16[336,6144]{1,0:T(8,128)(2,1)} %bitcast.12), kind=kOutput, calls=%fused_computation.1 | convolution fusion | flops 10586161152 | bytes 27426816 | tf_op jit(solution)/shard_map/dot_general | solution.py:10
  170.5 0.4 fusion.4
  170.9 0.6 copy.19
  171.6 0.5 reshape.30
  172.0 0.2 copy.22
  172.3 0.4 pad.4.clone
  172.7 0.0 copy-start.1
  172.7 1.3 reshape.31
  174.1 11.6 %all-to-all-start.1 = ((bf16[256,15,128]{2,1,0:T(8,128)(2,1)}), bf16[256,15,128]{2,1,0:T(8,128)(2,1)S(1)}, u32[]{:S(2)}, u32[]{:S(2)}) async-start(bf16[256,15,128]{2,1,0:T(8,128)(2,1)} %reshape.31), calls=%async_computation.1 | async-start | bytes 2097152 | tf_op jit(solution)/shard_map/all_to_all | solution.py:53
  185.7 0.1 reshape.36
  185.8 0.0 copy-done.1
  185.8 0.1 copy.15
  185.9 30.1 %all-to-all-done.1 = bf16[256,15,128]{2,1,0:T(8,128)(2,1)S(1)} async-done(((bf16[256,15,128]{2,1,0:T(8,128)(2,1)}), bf16[256,15,128]{2,1,0:T(8,128)(2,1)S(1)}, u32[]{:S(2)}, u32[]{:S(2)}) %all-to-all-start.1) | async-done | bytes 983072 | tf_op jit(solution)/shard_map/all_to_all | solution.py:53
  216.0 0.5 reshape.32
  216.5 0.2 slice_bitcast_fusion
  216.7 0.1 copy.21
  216.9 1.2 reshape.33
  218.1 1.0 gather_fusion
  219.1 0.3 reshape.44
  219.4 1.2 multiply_convert_fusion
  (2 shorter events, 0.0 us)
Async XLA Ops:
  6.5 1.4 copy-start
  6.5 148.4 %all-gather.2.cloned.1.call-start = ((), (), s32[]{:S(2)}) async-start(), calls=%async_computation.2 | async-start | bytes 16711680 | tf_op jit(solution)/shard_map/all_gather | solution.py:44
  172.7 13.1 %copy-start.1 = (f32[16,4]{0,1:T(4,128)S(1)}, f32[16,4]{0,1:T(4,128)}, u32[]{:S(2)}) copy-start(f32[16,4]{0,1:T(4,128)} %param.7) | copy-start | bytes 772
  174.1 42.0 %all-to-all-start.1 = ((bf16[256,15,128]{2,1,0:T(8,128)(2,1)}), bf16[256,15,128]{2,1,0:T(8,128)(2,1)S(1)}, u32[]{:S(2)}, u32[]{:S(2)}) async-start(bf16[256,15,128]{2,1,0:T(8,128)(2,1)} %reshape.31), calls=%async_computation.1 | async-start | bytes 2097152 | tf_op jit(solution)/shard_map/all_to_all | solution.py:53
Sparse Core Ops, SparseCore 0:
  47.3 107.6 all-gather.1

commit v12 on v11

--- a/solution.py
+++ b/solution.py
@@ -5,13 +5,15 @@
 
 
 def hidden_block(row_block, gate_rows, up_rows):
-    columns = gate_rows.shape[0]
-    both = jnp.concatenate([gate_rows, up_rows], axis=0)
+    columns, width = gate_rows.shape
+    wide = -(-columns // 128) * 128
+    pad = jnp.zeros((wide - columns, width), gate_rows.dtype)
+    both = jnp.concatenate([gate_rows, pad, up_rows, pad], axis=0)
     acts = lax.dot_general(
         row_block, both, (((1,), (1,)), ((), ())), preferred_element_type=jnp.float32
     )
-    gate_act = acts[:, :columns]
-    up_act = acts[:, columns:]
+    gate_act = acts[:, :wide]
+    up_act = acts[:, wide:]
     gelu = gate_act * (1.0 + lax.erf(gate_act * (2.0 ** -0.5))) * 0.5
     return (gelu * up_act).astype(jnp.bfloat16)
 
@@ -45,10 +47,9 @@
         gate_rows,
         up_rows,
     )
-    shaped = local_hidden.reshape(fsdp_size, experts, cap_slots, columns)
-    wide = -(-columns // 128) * 128
+    wide = local_hidden.shape[1]
+    shaped = local_hidden.reshape(fsdp_size, experts, cap_slots, wide)
     by_owner = jnp.transpose(shaped, (1, 0, 2, 3))
-    by_owner = jnp.pad(by_owner, ((0, 0), (0, 0), (0, 0), (0, wide - columns)))
     by_owner = by_owner.reshape(experts * fsdp_size, cap_slots * wide // 128, 128)
     returned = lax.all_to_all(by_owner, ("expert", "fsdp"), 0, 0, tiled=True)
     returned = returned.reshape(experts, fsdp_size, cap_slots, wide)[..., :columns]

time: 228 us -> 237 us (1.039)
  matrix products: 15.9 us -> 26.3 us
    dot_general x1, matrix products: 15.5 us -> 25.9 us  [hidden_block(): lax.dot_general(row_block, both, (((1,), (1,)), ((), ())), preferred_elem...]
where the time goes in v12:
time: 237 us
  waiting for transfers between devices  138 us (58%)
  blocking collectives  36.9 us (16%)
  matrix products  26.3 us (11%)
  between operations  13.5 us (6%)
  starting transfers between devices  11.6 us (5%)
  local copies, waits for them, and re-layouts  8.43 us (4%)
    all_gather x1, waiting for transfers between devices, local(): lax.all_gather(arrived.reshape(-1, model_width), 'fsdp', axis=0, tiled=True)  108 us
    all_to_all x1, blocking collectives, local(): lax.all_to_all(dense, 'expert', split_axis=0, concat_axis=0, tiled=True)  36.9 us
    all_to_all x1, waiting for transfers between devices, local(): returned = lax.all_to_all(by_owner, ('expert', 'fsdp'), 0, 0, tiled=True)  30.1 us
    dot_general x1, matrix products, hidden_block(): lax.dot_general(row_block, both, (((1,), (1,)), ((), ())), preferred_elem...  25.9 us
    all_to_all x1, starting transfers between devices, local(): returned = lax.all_to_all(by_owner, ('expert', 'fsdp'), 0, 0, tiled=True)  11.6 us
  transfers between devices with their start and end apart: 2, of which 2 were waited for; matrix products, arithmetic and copies ran while one was open for 0% of the time, Pallas kernels for 0%

profile of v12, /device:TPU:1, one launch (start us, length us, event | category | flops | bytes accessed | tf_op | source)
XLA Modules:
  0.0 236.7 jit_solution(16539372849012632182)
XLA Ops:
  6.5 0.0 copy-start
  6.5 0.0 all-gather.2.cloned.1.call-start
  6.5 0.8 copy.15
  7.3 0.1 eq.28
  7.4 0.2 convert_reduce_fusion
  7.6 0.1 reduce_sum.24
  7.7 0.1 copy.17
  7.8 0.1 fusion.11
  7.9 0.0 copy-done
  7.9 0.4 convolution_convert_fusion
  8.3 0.4 reshape_reshape.3
  8.8 36.9 %all_to_all.10 = bf16[16,240,128]{2,1,0:T(8,128)(2,1)S(1)} all-to-all(bf16[16,240,128]{2,1,0:T(8,128)(2,1)S(1)} %reshape_reshape.3), channel_id=1, replica_groups=mesh['expert'=16,'fsdp'=16] {'expert'}, dimensions={0} | all-to-all | bytes 1966080 | tf_op jit(solution)/shard_map/all_to_all | solution.py:44
  45.7 1.4 reshape.29
  47.1 0.0 all-gather.2.cloned.1.call-update
  47.1 107.8 %all-gather.2.cloned.1.call-done = bf16[1280,6144]{1,0:T(8,128)(2,1)} async-done(((bf16[80,6144]{1,0:T(8,128)(2,1)}), bf16[1280,6144]{1,0:T(8,128)(2,1)}) %all-gather.2.cloned.1.call-update) | async-done | bytes 15728656 | tf_op jit(solution)/shard_map/all_gather | solution.py:46
  155.0 25.9 %fusion = f32[1280,768]{1,0:T(8,128)S(1)} fusion(bf16[1280,6144]{1,0:T(8,128)(2,1)} %all-gather.2.cloned.1.call-done, bf16[48,6144]{1,0:T(8,128)(2,1)S(1)} %broadcast_in_dim.3, bf16[336,6144]{1,0:T(8,128)(2,1)} %bitcast.11, bf16[336,6144]{1,0:T(8,128)(2,1)} %bitcast.12), kind=kOutput, calls=%fused_computation.1 | convolution fusion | flops 12117344256 | bytes 28508160 | tf_op jit(solution)/shard_map/dot_general | solution.py:12
  180.9 0.5 fusion.8
  181.4 0.4 reshape.30
  181.8 0.0 copy-start.1
  181.8 0.2 copy.18
  182.0 1.3 reshape.31
  183.4 11.6 %all-to-all-start.1 = ((bf16[256,15,128]{2,1,0:T(8,128)(2,1)}), bf16[256,15,128]{2,1,0:T(8,128)(2,1)S(1)}, u32[]{:S(2)}, u32[]{:S(2)}) async-start(bf16[256,15,128]{2,1,0:T(8,128)(2,1)} %reshape.31), calls=%async_computation.1 | async-start | bytes 2097152 | tf_op jit(solution)/shard_map/all_to_all | solution.py:54
  195.0 0.1 reshape.36
  195.1 0.0 copy-done.1
  195.1 0.1 copy.14
  195.2 30.1 %all-to-all-done.1 = bf16[256,15,128]{2,1,0:T(8,128)(2,1)S(1)} async-done(((bf16[256,15,128]{2,1,0:T(8,128)(2,1)}), bf16[256,15,128]{2,1,0:T(8,128)(2,1)S(1)}, u32[]{:S(2)}, u32[]{:S(2)}) %all-to-all-start.1) | async-done | bytes 983072 | tf_op jit(solution)/shard_map/all_to_all | solution.py:54
  225.4 0.5 reshape.32
  225.9 0.2 slice_bitcast_fusion
  226.0 0.1 copy.19
  226.2 1.2 reshape.33
  227.4 1.0 gather_fusion
  228.4 0.3 reshape.44
  228.7 1.2 multiply_convert_fusion
  (3 shorter events, 0.1 us)
Async XLA Ops:
  6.5 1.4 copy-start
  6.5 148.4 %all-gather.2.cloned.1.call-start = ((), (), s32[]{:S(2)}) async-start(), calls=%async_computation.2 | async-start | bytes 16711680 | tf_op jit(solution)/shard_map/all_gather | solution.py:46
  181.8 13.3 %copy-start.1 = (f32[16,4]{0,1:T(4,128)S(1)}, f32[16,4]{0,1:T(4,128)}, u32[]{:S(2)}) copy-start(f32[16,4]{0,1:T(4,128)} %param.7) | copy-start | bytes 772
  183.4 42.0 %all-to-all-start.1 = ((bf16[256,15,128]{2,1,0:T(8,128)(2,1)}), bf16[256,15,128]{2,1,0:T(8,128)(2,1)S(1)}, u32[]{:S(2)}, u32[]{:S(2)}) async-start(bf16[256,15,128]{2,1,0:T(8,128)(2,1)} %reshape.31), calls=%async_computation.1 | async-start | bytes 2097152 | tf_op jit(solution)/shard_map/all_to_all | solution.py:54
Sparse Core Ops, SparseCore 0:
  47.3 107.6 all-gather.1

commit v13 on v11

--- a/solution.py
+++ b/solution.py
@@ -22,11 +22,11 @@
     experts = lax.axis_size("expert")
     fsdp_size = lax.axis_size("fsdp")
     cap_slots = 5 * tok_rows * top_count // (4 * experts)
-    flat_ids = expert_ids.reshape(-1)
+    flat_ids = expert_ids.T.reshape(-1)
     order = jnp.arange(flat_ids.shape[0], dtype=jnp.int32)
     earlier = (order[None, :] < order[:, None]) & (flat_ids[None, :] == flat_ids[:, None])
     slot_rank = jnp.sum(earlier.astype(jnp.int32), axis=1)
-    slot_of = flat_ids * cap_slots + slot_rank
+    slot_of = (flat_ids * cap_slots + slot_rank).reshape(top_count, tok_rows).T.reshape(-1)
     slots = jnp.arange(experts * cap_slots, dtype=jnp.int32)
     placing = (slot_of.reshape(tok_rows, top_count)[:, :, None] == slots).astype(jnp.bfloat16)
     by_token = jnp.sum(placing, axis=1)

time: 228 us -> 228 us (level)
  no operation moved by 1% of the time
where the time goes in v13:
time: 228 us
  waiting for transfers between devices  138 us (61%)
  blocking collectives  36.9 us (16%)
  matrix products  16 us (7%)
  between operations  13.5 us (6%)
  starting transfers between devices  11.6 us (5%)
  local copies, waits for them, and re-layouts  9.36 us (4%)
  other arithmetic  2.53 us (1%)
    all_gather x1, waiting for transfers between devices, local(): lax.all_gather(arrived.reshape(-1, model_width), 'fsdp', axis=0, tiled=True)  108 us
    all_to_all x1, blocking collectives, local(): lax.all_to_all(dense, 'expert', split_axis=0, concat_axis=0, tiled=True)  36.9 us
    all_to_all x1, waiting for transfers between devices, local(): returned = lax.all_to_all(by_owner, ('expert', 'fsdp'), 0, 0, tiled=True)  30.1 us
    dot_general x1, matrix products, hidden_block(): lax.dot_general(row_block, both, (((1,), (1,)), ((), ())), preferred_elem...  15.5 us
    all_to_all x1, starting transfers between devices, local(): returned = lax.all_to_all(by_owner, ('expert', 'fsdp'), 0, 0, tiled=True)  11.6 us
  transfers between devices with their start and end apart: 2, of which 2 were waited for; matrix products, arithmetic and copies ran while one was open for 0% of the time, Pallas kernels for 0%

profile of v13, /device:TPU:1, one launch (start us, length us, event | category | flops | bytes accessed | tf_op | source)
XLA Modules:
  0.0 227.8 jit_solution(15548242615643780807)
XLA Ops:
  6.5 0.0 copy-start
  6.5 0.0 all-gather.2.cloned.1.call-start
  6.5 0.8 eq.28
  7.3 0.2 convert_reduce_fusion
  7.5 0.1 reduce_sum.24
  7.6 0.7 add_bitcast_fusion
  8.3 0.1 fusion.7
  8.4 0.0 copy-done
  8.4 0.4 convolution_convert_fusion
  8.8 0.4 reshape_reshape.3
  9.3 36.9 %all_to_all.10 = bf16[16,240,128]{2,1,0:T(8,128)(2,1)S(1)} all-to-all(bf16[16,240,128]{2,1,0:T(8,128)(2,1)S(1)} %reshape_reshape.3), channel_id=1, replica_groups=mesh['expert'=16,'fsdp'=16] {'expert'}, dimensions={0} | all-to-all | bytes 1966080 | tf_op jit(solution)/shard_map/all_to_all | solution.py:42
  46.2 1.4 reshape.22
  47.6 0.0 all-gather.2.cloned.1.call-update
  47.6 107.8 %all-gather.2.cloned.1.call-done = bf16[1280,6144]{1,0:T(8,128)(2,1)} async-done(((bf16[80,6144]{1,0:T(8,128)(2,1)}), bf16[1280,6144]{1,0:T(8,128)(2,1)}) %all-gather.2.cloned.1.call-update) | async-done | bytes 15728656 | tf_op jit(solution)/shard_map/all_gather | solution.py:44
  155.5 15.5 %fusion = f32[1280,672]{0,1:T(8,128)S(1)} fusion(bf16[1280,6144]{1,0:T(8,128)(2,1)} %all-gather.2.cloned.1.call-done, bf16[336,6144]{1,0:T(8,128)(2,1)} %bitcast.16, bf16[336,6144]{1,0:T(8,128)(2,1)} %bitcast.17), kind=kOutput, calls=%fused_computation.1 | convolution fusion | flops 10586161152 | bytes 27426816 | tf_op jit(solution)/shard_map/dot_general | solution.py:10
  171.0 0.4 fusion.4
  171.4 0.6 copy.16
  172.1 0.5 reshape.23
  172.6 0.2 copy.20
  172.8 0.4 pad.4.clone
  173.2 0.0 copy-start.1
  173.2 1.3 reshape.24
  174.5 11.6 %all-to-all-start.1 = ((bf16[256,15,128]{2,1,0:T(8,128)(2,1)}), bf16[256,15,128]{2,1,0:T(8,128)(2,1)S(1)}, u32[]{:S(2)}, u32[]{:S(2)}) async-start(bf16[256,15,128]{2,1,0:T(8,128)(2,1)} %reshape.24), calls=%async_computation.1 | async-start | bytes 2097152 | tf_op jit(solution)/shard_map/all_to_all | solution.py:53
  186.2 0.1 copy.19
  186.2 0.1 reshape.29
  186.3 0.0 copy-done.1
  186.3 0.1 copy.15
  186.4 30.1 %all-to-all-done.1 = bf16[256,15,128]{2,1,0:T(8,128)(2,1)S(1)} async-done(((bf16[256,15,128]{2,1,0:T(8,128)(2,1)}), bf16[256,15,128]{2,1,0:T(8,128)(2,1)S(1)}, u32[]{:S(2)}, u32[]{:S(2)}) %all-to-all-start.1) | async-done | bytes 983072 | tf_op jit(solution)/shard_map/all_to_all | solution.py:53
  216.5 0.5 reshape.25
  217.0 0.2 slice_bitcast_fusion
  217.2 0.1 copy.18
  217.3 1.2 reshape.26
  218.5 1.0 gather_fusion
  219.5 0.3 reshape.37
  219.8 1.2 multiply_convert_fusion
  (1 shorter events, 0.0 us)
Async XLA Ops:
  6.5 1.9 copy-start
  6.5 148.9 %all-gather.2.cloned.1.call-start = ((), (), s32[]{:S(2)}) async-start(), calls=%async_computation.2 | async-start | bytes 16711680 | tf_op jit(solution)/shard_map/all_gather | solution.py:44
  173.2 13.2 %copy-start.1 = (f32[16,4]{0,1:T(4,128)S(1)}, f32[16,4]{0,1:T(4,128)}, u32[]{:S(2)}) copy-start(f32[16,4]{0,1:T(4,128)} %param.7) | copy-start | bytes 772
  174.5 42.0 %all-to-all-start.1 = ((bf16[256,15,128]{2,1,0:T(8,128)(2,1)}), bf16[256,15,128]{2,1,0:T(8,128)(2,1)S(1)}, u32[]{:S(2)}, u32[]{:S(2)}) async-start(bf16[256,15,128]{2,1,0:T(8,128)(2,1)} %reshape.24), calls=%async_computation.1 | async-start | bytes 2097152 | tf_op jit(solution)/shard_map/all_to_all | solution.py:53
Sparse Core Ops, SparseCore 0:
  47.8 107.6 all-gather.1
